TPU v7x, 256 devices: a whole 4x4x8 slice. The times are simulated.
256 devices in a mesh: dp: 64 (over x, z, core), tensor: 4 (over y).
Axes of the slice: x: 4, y: 4, z: 8, core: 2. Of those that a mesh axis runs over, the one named last changes fastest.
Arguments:
- attention_grads: bfloat16 [64, 1, 512, 2048], P('dp', None, None, 'tensor')
- expert_grads: bfloat16 [64, 1, 2, 512, 4096], P('dp', None, None, None, 'tensor')
- routing_grads: bfloat16 [64, 4, 1, 36, 512], P('dp', 'tensor'), may hold values from -640 to 640
- attention_master: float32 [512, 2048], P('dp', 'tensor'), may hold values from -0.25 to 0.25
- attention_first: float32 [512, 2048], P('dp', 'tensor'), may hold values from -4 to 4
- attention_second: float32 [512, 2048], P('dp', 'tensor'), may hold values from 0.05 to 2
- expert_master: float32 [2, 512, 4096], P(None, 'dp', 'tensor'), may hold values from -0.25 to 0.25
- expert_first: float32 [2, 512, 4096], P(None, 'dp', 'tensor'), may hold values from -4 to 4
- expert_second: float32 [2, 512, 4096], P(None, 'dp', 'tensor'), may hold values from 0.05 to 2
- routing_master: float32 [36, 512], P(None, ('dp', 'tensor')), may hold values from -4 to 4
- routing_first: float32 [36, 512], P(None, ('dp', 'tensor')), may hold values from -4 to 4
- routing_second: float32 [36, 512], P(None, ('dp', 'tensor')), may hold values from 0.05 to 2
- step_count: int32 [1], replicated, may hold values from 1 to 1000
- learn_rate: float32 [1], replicated, may hold values from 0.05 to 0.3
- clip_level: float32 [1], replicated, may hold values from 0.5 to 2
Outputs:
- attention_renewed: float32 [512, 2048], P('dp', 'tensor')
- attention_momentum: float32 [512, 2048], P('dp', 'tensor')
- attention_variance: float32 [512, 2048], P('dp', 'tensor')
- attention_served: bfloat16 [512, 2048], P(None, 'tensor')
- expert_renewed: float32 [2, 512, 4096], P(None, 'dp', 'tensor')
- expert_momentum: float32 [2, 512, 4096], P(None, 'dp', 'tensor')
- expert_variance: float32 [2, 512, 4096], P(None, 'dp', 'tensor')
- expert_served: bfloat16 [2, 512, 4096], P(None, None, 'tensor')
- routing_renewed: float32 [36, 512], P(None, ('dp', 'tensor'))
- routing_momentum: float32 [36, 512], P(None, ('dp', 'tensor'))
- routing_variance: float32 [36, 512], P(None, ('dp', 'tensor'))
- routing_served: bfloat16 [36, 512], replicated
Inputs may be any that keep to these rules, and one draw needn't show every extreme that they name: `step_count`: the number of optimizer steps taken, this one included.
All inputs are finite; a program needn't handle non-finite values.
Results may differ from a plain program's by a relative error of at most 0.0004.
Values may be sent and summed in bfloat16 or wider, within the bound.
No kernel may reach another device: no remote copies, remote signals or barrier semaphores. Data moves between devices by JAX's collectives and lax.ppermute only.
A program may use at most 64 MiB of HBM per device.

v0:
```python
from functools import reduce

import jax
import jax.numpy as jnp
from jax import lax
from jax.sharding import PartitionSpec as P

EXPERTS = 32
PARAMS = 5261312


BETA_ONE = 0.9
BETA_TWO = 0.999
EPSILON = 1e-08
DECAY = 0.1


def micro_total(blocks):
    return reduce(lambda left, right: left + right, [blocks[0].astype(jnp.float32)])


def adam_update(grad_sum, master, first, second, clip, rate, first_fix, second_fix, mask):
    grad = clip * grad_sum
    momentum = BETA_ONE * first + (1.0 - BETA_ONE) * grad
    variance = BETA_TWO * second + (1.0 - BETA_TWO) * grad * grad
    update = (
        momentum / first_fix / (jnp.sqrt(variance / second_fix) + EPSILON) + DECAY * mask * master
    )
    renewed = master - rate * update
    return (renewed, momentum, variance, renewed.astype(jnp.bfloat16))


def local(
    attention_grads,
    expert_grads,
    routing_grads,
    attention_master,
    attention_first,
    attention_second,
    expert_master,
    expert_first,
    expert_second,
    routing_master,
    routing_first,
    routing_second,
    step_count,
    learn_rate,
    clip_level,
):
    attention_local = attention_grads[0]
    expert_local = expert_grads[0]
    attention_sum = lax.psum_scatter(
        micro_total(attention_local), "dp", scatter_dimension=0, tiled=True
    )
    expert_sum = lax.psum_scatter(micro_total(expert_local), "dp", scatter_dimension=1, tiled=True)
    expert_pieces = [expert_sum[index] for index in range(expert_sum.shape[0])]
    routing_local = micro_total(routing_grads[0, 0])
    routing_sum = lax.psum_scatter(routing_local, ("dp", "tensor"), scatter_dimension=1, tiled=True)
    expert_squares = reduce(
        lambda left, right: left + right, [jnp.sum(piece * piece) for piece in expert_pieces]
    )
    attention_total, expert_total, routing_total = lax.psum(
        (
            jnp.sum(attention_sum * attention_sum),
            expert_squares,
            jnp.sum(routing_sum * routing_sum),
        ),
        ("dp", "tensor"),
    )
    grad_norm = jnp.sqrt(attention_total + expert_total + routing_total)
    clip = jnp.minimum(1.0, clip_level[0] * jnp.sqrt(jnp.float32(PARAMS)) / (grad_norm + 1e-06))
    steps_done = step_count[0].astype(jnp.float32)
    first_fix = 1.0 - jnp.power(jnp.float32(BETA_ONE), steps_done)
    second_fix = 1.0 - jnp.power(jnp.float32(BETA_TWO), steps_done)
    rate = learn_rate[0]
    attention_out = adam_update(
        attention_sum,
        attention_master,
        attention_first,
        attention_second,
        clip,
        rate,
        first_fix,
        second_fix,
        jnp.float32(1.0),
    )
    attention_served = lax.all_gather(attention_out[3], "dp", axis=0, tiled=True)
    expert_sum = jnp.stack(expert_pieces, axis=0)
    expert_out = adam_update(
        expert_sum,
        expert_master,
        expert_first,
        expert_second,
        clip,
        rate,
        first_fix,
        second_fix,
        jnp.float32(1.0),
    )
    expert_renewed, expert_momentum, expert_variance = (expert_out[0], expert_out[1], expert_out[2])
    expert_served = lax.all_gather(expert_out[3], "dp", axis=1, tiled=True)
    row_index = jnp.arange(routing_master.shape[0], dtype=jnp.int32)
    routing_mask = (row_index < EXPERTS).astype(jnp.float32)[:, None]
    routing_out = adam_update(
        routing_sum,
        routing_master,
        routing_first,
        routing_second,
        clip,
        rate,
        first_fix,
        second_fix,
        routing_mask,
    )
    routing_served = lax.all_gather(routing_out[3], ("dp", "tensor"), axis=1, tiled=True)
    return (
        attention_out[0],
        attention_out[1],
        attention_out[2],
        attention_served,
        expert_renewed,
        expert_momentum,
        expert_variance,
        expert_served,
        routing_out[0],
        routing_out[1],
        routing_out[2],
        routing_served,
    )


def solution(mesh):
    in_specs = (
        P("dp", None, None, "tensor"),
        P("dp", None, None, None, "tensor"),
        P("dp", "tensor", None, None, None),
        P("dp", "tensor"),
        P("dp", "tensor"),
        P("dp", "tensor"),
        P(None, "dp", "tensor"),
        P(None, "dp", "tensor"),
        P(None, "dp", "tensor"),
        P(None, ("dp", "tensor")),
        P(None, ("dp", "tensor")),
        P(None, ("dp", "tensor")),
        P(),
        P(),
        P(),
    )
    out_specs = (
        P("dp", "tensor"),
        P("dp", "tensor"),
        P("dp", "tensor"),
        P(None, "tensor"),
        P(None, "dp", "tensor"),
        P(None, "dp", "tensor"),
        P(None, "dp", "tensor"),
        P(None, None, "tensor"),
        P(None, ("dp", "tensor")),
        P(None, ("dp", "tensor")),
        P(None, ("dp", "tensor")),
        P(),
    )
    return jax.shard_map(local, mesh=mesh, in_specs=in_specs, out_specs=out_specs, check_vma=False)
```

profile of v0, /device:TPU:4, one launch (start us, length us, event | category | flops | bytes accessed | tf_op | source)
XLA Modules:
  0.0 541.3 jit_solution(8500737560989414469)
XLA Ops:
  8.0 0.0 copy-start
  8.0 0.0 all-reduce.3.cloned.1.call-start
  8.1 1.1 copy.29
  9.1 0.7 bitcast_convert_fusion.2
  9.9 0.0 all-reduce.3.cloned.1.call-update
  9.9 0.0 reduce-scatter.3.cloned.1.call-start
  9.9 2.1 bitcast_convert_fusion.1
  12.1 0.0 reduce-scatter.3.cloned.1.call-update
  12.1 0.0 reduce-scatter.5.cloned.1.call-start
  12.2 0.0 copy-done
  12.2 2.4 bitcast_convert_fusion
  14.6 0.0 copy-start.1
  14.6 0.0 copy-start.2
  14.6 0.0 copy-start.3
  14.6 0.0 copy-start.7
  14.6 0.0 copy-start.8
  14.6 0.0 copy-start.9
  14.6 0.0 copy-start.4
  14.6 0.0 copy-start.5
  14.6 0.0 copy-start.6
  14.6 0.0 reduce-scatter.5.cloned.1.call-update
  14.7 0.0 all-gather.3.cloned.1.call-start
  16.8 257.2 %all-reduce.3.cloned.1.call-done = f32[36,512]{0,1:T(8,128)} async-done(((f32[36,512]{0,1:T(8,128)}), f32[36,512]{0,1:T(8,128)}) %all-reduce.3.cloned.1.call-update) | async-done | bytes 73744
  273.9 1.3 multiply_reduce_fusion.1
  275.2 0.0 reduce-scatter.3.cloned.1.call-done
  275.2 1.3 multiply_reduce_fusion
  276.6 27.6 %reduce-scatter.5.cloned.1.call-done = f32[2,8,1024]{2,1,0:T(8,128)} async-done(((f32[2,512,1024]{2,1,0:T(8,128)}), f32[2,8,1024]{2,1,0:T(8,128)}) %reduce-scatter.5.cloned.1.call-update) | async-done | bytes 65552 | tf_op jit(solution)/shard_map/reduce_scatter | solution.py:55
  304.1 1.4 fusion.1
  308.1 73.6 %psum.25 = f32[]{:T(128)} all-reduce(f32[]{:T(128)S(6)} %add.71), channel_id=1, replica_groups=mesh['dp'=64,'tensor'=4] {'dp','tensor'}, use_global_device_ids=true, to_apply=%region_2.0 | all-reduce | flops 1 | bytes 8 | tf_op jit(solution)/shard_map/psum | solution.py:62
  382.4 0.0 copy-done.1
  382.4 0.0 copy-done.2
  382.5 0.0 copy-done.3
  382.5 1.5 fusion.6
  384.0 0.0 all-gather.3.cloned.1.call-update
  384.0 0.0 copy-done.7
  384.1 0.0 copy-done.8
  384.1 0.0 copy-done.9
  384.1 1.3 convert_bitcast_fusion
  385.4 94.1 %all-gather = bf16[256,2,36]{2,1,0:T(2,128)(2,1)S(1)} all-gather(bf16[1,2,36]{2,1,0:T(2,128)(2,1)S(1)} %get-tuple-element.14), channel_id=1, replica_groups=mesh['dp'=64,'tensor'=4] {'dp','tensor'}, dimensions={0}, use_global_device_ids=true | all-gather | bytes 37008 | tf_op jit(solution)/shard_map/all_gather | solution.py:115
  479.5 0.7 copy.30
  480.2 0.0 copy-done.4
  480.2 0.0 copy-done.5
  480.2 0.0 copy-done.6
  480.2 1.4 fusion.8
  481.6 48.2 %all_gather.9 = bf16[512,512]{1,0:T(8,128)(2,1)S(1)} all-gather(bf16[8,512]{1,0:T(8,128)(2,1)S(1)} %get-tuple-element.22), channel_id=1, replica_groups=mesh['dp'=64,'tensor'=4] {'dp'}, dimensions={0}, use_global_device_ids=true | all-gather | bytes 532480 | tf_op jit(solution)/shard_map/all_gather | solution.py:87
  529.8 0.0 all-gather.3.cloned.1.call-done
  529.8 0.8 copy.37
  530.6 3.1 copy.38
  (1 shorter events, 0.0 us)
Async XLA Ops:
  8.0 4.1 copy-start
  8.0 265.9 %all-reduce.3.cloned.1.call-start = ((), (), s32[]{:S(2)}) async-start(), calls=%async_computation.5 | async-start | bytes 524288
  9.9 265.4 %reduce-scatter.3.cloned.1.call-start = ((), (), s32[]{:S(2)}) async-start(), calls=%async_computation.2 | async-start | bytes 1064960 | tf_op jit(solution)/shard_map/reduce_scatter | solution.py:52
  12.1 292.0 %reduce-scatter.5.cloned.1.call-start = ((), (), s32[]{:S(2)}) async-start(), calls=%async_computation.3 | async-start | bytes 4259840 | tf_op jit(solution)/shard_map/reduce_scatter | solution.py:55
  14.6 367.9 %copy-start.1 = (f32[2,8,1024]{2,1,0:T(8,128)S(1)}, f32[2,8,1024]{2,1,0:T(8,128)}, u32[]{:S(2)}) copy-start(f32[2,8,1024]{2,1,0:T(8,128)} %param.21) | copy-start | bytes 196612
  14.6 367.9 %copy-start.2 = (f32[2,8,1024]{2,1,0:T(8,128)S(1)}, f32[2,8,1024]{2,1,0:T(8,128)}, u32[]{:S(2)}) copy-start(f32[2,8,1024]{2,1,0:T(8,128)} %param.23) | copy-start | bytes 196612
  14.6 367.9 %copy-start.3 = (f32[2,8,1024]{2,1,0:T(8,128)S(1)}, f32[2,8,1024]{2,1,0:T(8,128)}, u32[]{:S(2)}) copy-start(f32[2,8,1024]{2,1,0:T(8,128)} %param.22) | copy-start | bytes 196612
  14.6 369.5 %copy-start.7 = (f32[36,2]{0,1:T(2,128)S(1)}, f32[36,2]{0,1:T(2,128)}, u32[]{:S(2)}) copy-start(f32[36,2]{0,1:T(2,128)} %param.24) | copy-start | bytes 868
  14.6 369.5 %copy-start.8 = (f32[36,2]{0,1:T(2,128)S(1)}, f32[36,2]{0,1:T(2,128)}, u32[]{:S(2)}) copy-start(f32[36,2]{0,1:T(2,128)} %param.26) | copy-start | bytes 868
  14.6 369.5 %copy-start.9 = (f32[36,2]{0,1:T(2,128)S(1)}, f32[36,2]{0,1:T(2,128)}, u32[]{:S(2)}) copy-start(f32[36,2]{0,1:T(2,128)} %param.25) | copy-start | bytes 868
  14.6 465.6 %copy-start.4 = (f32[8,512]{1,0:T(8,128)S(1)}, f32[8,512]{1,0:T(8,128)}, u32[]{:S(2)}) copy-start(f32[8,512]{1,0:T(8,128)} %param.18) | copy-start | bytes 49156
  14.6 465.6 %copy-start.5 = (f32[8,512]{1,0:T(8,128)S(1)}, f32[8,512]{1,0:T(8,128)}, u32[]{:S(2)}) copy-start(f32[8,512]{1,0:T(8,128)} %param.20) | copy-start | bytes 49156
  14.6 465.6 %copy-start.6 = (f32[8,512]{1,0:T(8,128)S(1)}, f32[8,512]{1,0:T(8,128)}, u32[]{:S(2)}) copy-start(f32[8,512]{1,0:T(8,128)} %param.19) | copy-start | bytes 49156
  14.7 515.1 %all-gather.3.cloned.1.call-start = ((), (), s32[]{:S(2)}) async-start(), calls=%async_computation.4 | async-start | bytes 2129920 | tf_op jit(solution)/shard_map/all_gather | solution.py:101
Sparse Core Ops, SparseCore 0:
  14.9 259.0 all-reduce.2
Sparse Core Ops, SparseCore 1:
  14.9 142.4 reduce-scatter.2
  161.4 142.7 reduce-scatter.4
  384.1 74.5 all-gather.2
where the time goes:
time: 544 us; the launch traced here: 541 us
  waiting for transfers between devices  285 us (52%)
  blocking collectives  216 us (40%)
  between operations  21.2 us (4%)
  other arithmetic  13.4 us (2%)
  local copies, waits for them, and re-layouts  5.73 us (1%)
    unnamed x5, waiting for transfers between devices  257 us
    all_gather x1, blocking collectives, local(): lax.all_gather(routing_out[3], ('dp', 'tensor'), axis=1, tiled=True)  94.1 us
    psum x1, blocking collectives, local(): lax.psum((jnp.sum(attention_sum * attention_sum), expert_squares, jnp.sum...  73.6 us
    all_gather x1, blocking collectives, local(): lax.all_gather(attention_out[3], 'dp', axis=0, tiled=True)  48.2 us
    reduce_scatter x1, waiting for transfers between devices, local(): lax.psum_scatter(micro_total(expert_local), 'dp', scatter_dimension=1, ti...  27.6 us
  transfers between devices with their start and end apart: 4, of which 2 were waited for; matrix products, arithmetic and copies ran while one was open for 2% of the time, Pallas kernels for 0%

commit v1 on v0

v1 whole, which is shorter than its diff:
```python
import jax
import jax.numpy as jnp
from jax import lax
from jax.sharding import PartitionSpec as P

EXPERTS = 32
PARAMS = 5261312


BETA_ONE = 0.9
BETA_TWO = 0.999
EPSILON = 1e-08
DECAY = 0.1


def adam_update(grad_sum, master, first, second, clip, rate, first_fix, second_fix, mask):
    grad = clip * grad_sum
    momentum = BETA_ONE * first + (1.0 - BETA_ONE) * grad
    variance = BETA_TWO * second + (1.0 - BETA_TWO) * grad * grad
    update = (
        momentum / first_fix / (jnp.sqrt(variance / second_fix) + EPSILON) + DECAY * mask * master
    )
    renewed = master - rate * update
    return (renewed, momentum, variance, renewed.astype(jnp.bfloat16))


def local(
    attention_grads,
    expert_grads,
    routing_grads,
    attention_master,
    attention_first,
    attention_second,
    expert_master,
    expert_first,
    expert_second,
    routing_master,
    routing_first,
    routing_second,
    step_count,
    learn_rate,
    clip_level,
):
    n_dp = lax.axis_size("dp")
    n_t = lax.axis_size("tensor")
    t_idx = lax.axis_index("tensor")

    att = attention_grads[0, 0]
    exp = expert_grads[0, 0]
    rte = routing_grads[0, 0, 0]
    rows, cols = att.shape
    n_e, e_rows, e_cols = exp.shape
    n_r, r_cols = rte.shape
    ra = rows // n_dp
    re = e_rows // n_dp
    rc = r_cols // n_dp
    own = rc // n_t

    att_blocks = att.reshape(n_dp, ra * cols)
    exp_blocks = exp.reshape(n_e, n_dp, re, e_cols).transpose(1, 0, 2, 3).reshape(n_dp, -1)
    rte_blocks = rte.reshape(n_r, n_dp, rc).transpose(1, 0, 2).reshape(n_dp, -1)
    send = jnp.concatenate([att_blocks, exp_blocks, rte_blocks], axis=1)
    got = lax.all_to_all(send, "dp", 0, 0, tiled=True)
    total = jnp.sum(got.astype(jnp.float32), axis=0)
    n_att = ra * cols
    n_exp = n_e * re * e_cols
    attention_sum = total[:n_att].reshape(ra, cols)
    expert_sum = total[n_att : n_att + n_exp].reshape(n_e, re, e_cols)
    route_part = total[n_att + n_exp :].reshape(n_r, rc)

    local_squares = jnp.sum(attention_sum * attention_sum) + jnp.sum(expert_sum * expert_sum)
    slot = (jnp.arange(rc) // own == t_idx)[None, :]

    def placed(values):
        return jnp.where(slot, jnp.tile(values, (1, n_t)), 0.0)

    packed = jnp.stack(
        [
            route_part,
            placed(routing_master),
            placed(routing_first),
            placed(routing_second),
            jnp.full((n_r, rc), 0.0).at[0, 0].set(local_squares),
        ]
    )
    packed = lax.psum(packed, "tensor")
    route_sum = packed[0]
    route_master_blk, route_first_blk, route_second_blk = packed[1], packed[2], packed[3]
    group_squares = packed[4, 0, 0] + jnp.sum(route_sum * route_sum)

    spread = jnp.broadcast_to(group_squares, (n_dp, 1))
    squares = jnp.sum(lax.all_to_all(spread, "dp", 0, 0, tiled=True))

    grad_norm = jnp.sqrt(squares)
    clip = jnp.minimum(1.0, clip_level[0] * jnp.sqrt(jnp.float32(PARAMS)) / (grad_norm + 1e-06))
    steps_done = step_count[0].astype(jnp.float32)
    first_fix = 1.0 - jnp.power(jnp.float32(BETA_ONE), steps_done)
    second_fix = 1.0 - jnp.power(jnp.float32(BETA_TWO), steps_done)
    rate = learn_rate[0]
    one = jnp.float32(1.0)
    attention_out = adam_update(
        attention_sum, attention_master, attention_first, attention_second,
        clip, rate, first_fix, second_fix, one,
    )
    expert_out = adam_update(
        expert_sum, expert_master, expert_first, expert_second,
        clip, rate, first_fix, second_fix, one,
    )
    row_index = jnp.arange(n_r, dtype=jnp.int32)
    routing_mask = (row_index < EXPERTS).astype(jnp.float32)[:, None]
    routing_out = adam_update(
        route_sum, route_master_blk, route_first_blk, route_second_blk,
        clip, rate, first_fix, second_fix, routing_mask,
    )

    def mine(values):
        return lax.dynamic_slice_in_dim(values, t_idx * own, own, axis=1)

    served = jnp.concatenate(
        [
            attention_out[3].reshape(-1),
            expert_out[3].reshape(-1),
            routing_out[3].reshape(-1),
        ]
    )
    gathered = lax.all_to_all(jnp.broadcast_to(served, (n_dp,) + served.shape), "dp", 0, 0, tiled=True)
    attention_served = gathered[:, :n_att].reshape(rows, cols)
    expert_served = (
        gathered[:, n_att : n_att + n_exp]
        .reshape(n_dp, n_e, re, e_cols)
        .transpose(1, 0, 2, 3)
        .reshape(n_e, e_rows, e_cols)
    )
    routing_served = (
        gathered[:, n_att + n_exp :].reshape(n_dp, n_r, rc).transpose(1, 0, 2).reshape(n_r, r_cols)
    )
    return (
        attention_out[0],
        attention_out[1],
        attention_out[2],
        attention_served,
        expert_out[0],
        expert_out[1],
        expert_out[2],
        expert_served,
        mine(routing_out[0]),
        mine(routing_out[1]),
        mine(routing_out[2]),
        routing_served,
    )


def solution(mesh):
    in_specs = (
        P("dp", None, None, "tensor"),
        P("dp", None, None, None, "tensor"),
        P("dp", "tensor", None, None, None),
        P("dp", "tensor"),
        P("dp", "tensor"),
        P("dp", "tensor"),
        P(None, "dp", "tensor"),
        P(None, "dp", "tensor"),
        P(None, "dp", "tensor"),
        P(None, ("dp", "tensor")),
        P(None, ("dp", "tensor")),
        P(None, ("dp", "tensor")),
        P(),
        P(),
        P(),
    )
    out_specs = (
        P("dp", "tensor"),
        P("dp", "tensor"),
        P("dp", "tensor"),
        P(None, "tensor"),
        P(None, "dp", "tensor"),
        P(None, "dp", "tensor"),
        P(None, "dp", "tensor"),
        P(None, None, "tensor"),
        P(None, ("dp", "tensor")),
        P(None, ("dp", "tensor")),
        P(None, ("dp", "tensor")),
        P(),
    )
    return jax.shard_map(local, mesh=mesh, in_specs=in_specs, out_specs=out_specs, check_vma=False)
```

time: 544 us -> 320 us (0.59)
  blocking collectives: 216 us -> 17.3 us
  waiting for transfers between devices: 285 us -> 125 us
  local copies, waits for them, and re-layouts: 5.73 us -> 67.2 us
  other arithmetic: 13.4 us -> 71.7 us
  starting transfers between devices: 0.17 us -> 27.4 us
  between operations: 21.2 us -> 6.28 us
    unnamed x5 -> x0, waiting for transfers between devices: 257 us -> none
    all_gather x2 -> x0, blocking collectives: 142 us -> none  [the longest x1 94.1 us: local(): lax.all_gather(routing_out[3], ('dp', 'tensor'), axis=1, tiled=True)]
    all_to_all x0 -> x3, waiting for transfers between devices: none -> 125 us  [the longest x1 59.6 us: local(): lax.all_to_all(jnp.broadcast_to(served, (n_dp,) + served.shape), 'dp', 0,...]
    psum x1, blocking collectives: 73.6 us -> 17.3 us  [local(): packed = lax.psum(packed, 'tensor')]
    broadcast_in_dim x0 -> x1, other arithmetic: none -> 55.7 us  [local(): jnp.broadcast_to(served, (n_dp,) + served.shape)]
    reduce_scatter x2 -> x0, waiting for transfers between devices: 27.6 us -> none  [the longest x1 27.6 us: local(): lax.psum_scatter(micro_total(expert_local), 'dp', scatter_dimension=1, ti...]
    all_to_all x0 -> x3, starting transfers between devices: none -> 27.4 us  [the longest x1 12.1 us: local(): got = lax.all_to_all(send, 'dp', 0, 0, tiled=True)]
    unnamed x24 -> x28, local copies, waits for them, and re-layouts: 5.73 us -> 28.6 us
  transfers between devices with their start and end apart: 4 -> 3, of which waited for: 2 -> 3; matrix products, arithmetic and copies ran while one was open for 2% -> 1% of each run, Pallas kernels for 0% -> 0%
where the time goes in v1:
time: 320 us; the launch traced here: 315 us
  waiting for transfers between devices  125 us (39%)
  other arithmetic  71.7 us (22%)
  local copies, waits for them, and re-layouts  67.2 us (21%)
  starting transfers between devices  27.4 us (9%)
  blocking collectives  17.3 us (5%)
  between operations  6.28 us (2%)
    all_to_all x1, waiting for transfers between devices, local(): lax.all_to_all(jnp.broadcast_to(served, (n_dp,) + served.shape), 'dp', 0,...  59.6 us
    all_to_all x1, waiting for transfers between devices, local(): got = lax.all_to_all(send, 'dp', 0, 0, tiled=True)  58.5 us
    broadcast_in_dim x1, other arithmetic, local(): jnp.broadcast_to(served, (n_dp,) + served.shape)  55.7 us
    unnamed x28, local copies, waits for them, and re-layouts  28.6 us
    psum x1, blocking collectives, local(): packed = lax.psum(packed, 'tensor')  17.3 us
    all_to_all x1, local copies, waits for them, and re-layouts, local(): lax.all_to_all(jnp.broadcast_to(served, (n_dp,) + served.shape), 'dp', 0,...  13.3 us
    all_to_all x1, starting transfers between devices, local(): got = lax.all_to_all(send, 'dp', 0, 0, tiled=True)  12.1 us
    all_to_all x1, starting transfers between devices, local(): squares = jnp.sum(lax.all_to_all(spread, 'dp', 0, 0, tiled=True))  8.54 us
  transfers between devices with their start and end apart: 3, of which 3 were waited for; matrix products, arithmetic and copies ran while one was open for 1% of the time, Pallas kernels for 0%

profile of v1, /device:TPU:4, one launch (start us, length us, event | category | flops | bytes accessed | tf_op | source)
XLA Modules:
  0.0 315.0 jit_solution(10063507066040391948)
XLA Ops:
  0.6 0.9 copy.90
  1.6 0.2 copy.91
  1.7 0.1 copy.92
  1.8 1.3 reshape_squeeze.9
  3.1 1.8 copy.89
  4.9 1.3 copy.110
  6.2 0.2 maximum_bitcast_fusion
  6.4 0.5 broadcast.225
  6.9 3.4 %reduce.8 = bf16[64,20768]{1,0:T(8,128)(2,1)} reduce(bf16[64,1,20768]{2,0,1:T(8,128)(2,1)S(1)} %maximum_bitcast_fusion, bf16[]{:T(256)} %broadcast.225), dimensions={1}, to_apply=%copy.93.reduce_sub_computation | reduce | bytes 5316610 | tf_op jit(solution)/shard_map/all_to_all | solution.py:63
  10.3 5.6 %reshape.270 = bf16[64,2,10384]{2,1,0:T(2,128)(2,1)} reshape(bf16[64,20768]{1,0:T(8,128)(2,1)} %reduce.8) | data formatting | bytes 5316608
  15.8 12.1 %all-to-all-start = ((bf16[64,2,10384]{2,1,0:T(2,128)(2,1)}), bf16[64,2,10384]{2,1,0:T(2,128)(2,1)S(1)}, u32[]{:S(2)}, u32[]{:S(2)}) async-start(bf16[64,2,10384]{2,1,0:T(2,128)(2,1)} %reshape.270), calls=%async_computation | async-start | bytes 5373952 | tf_op jit(solution)/shard_map/all_to_all | solution.py:63
  30.0 0.1 mul.261
  30.1 58.5 %all-to-all-done = bf16[64,2,10384]{2,1,0:T(2,128)(2,1)S(1)} async-done(((bf16[64,2,10384]{2,1,0:T(2,128)(2,1)}), bf16[64,2,10384]{2,1,0:T(2,128)(2,1)S(1)}, u32[]{:S(2)}, u32[]{:S(2)}) %all-to-all-start) | async-done | bytes 2658336 | tf_op jit(solution)/shard_map/all_to_all | solution.py:63
  88.7 8.0 %reshape.271 = bf16[64,1,20768]{2,1,0:T(2,128)(2,1)} reshape(bf16[64,2,10384]{2,1,0:T(2,128)(2,1)S(1)} %all-to-all-done) | data formatting | bytes 5316608
  96.8 8.2 %convert_reduce_fusion = f32[20768]{0:T(1024)S(1)} fusion(bf16[64,1,20768]{2,1,0:T(2,128)(2,1)} %reshape.271), kind=kLoop, calls=%fused_computation | loop fusion | flops 2637536 | bytes 2741376 | tf_op jit(solution)/shard_map/reduce_sum | solution.py:64
  105.0 0.6 multiply_reduce_fusion
  105.6 0.6 multiply_reduce_fusion.1
  108.0 17.3 %psum.7 = f32[5,36,8]{1,2,0:T(8,128)S(1)} all-reduce(f32[5,36,8]{1,2,0:T(8,128)S(1)} %constant_dynamic-update-slice_fusion), channel_id=1, replica_groups=mesh['dp'=64,'tensor'=4] {'tensor'}, use_global_device_ids=true, to_apply=%region_3.4 | all-reduce | flops 1440 | bytes 11520 | tf_op jit(solution)/shard_map/psum | solution.py:86
  125.3 0.5 slice.63
  125.8 0.6 slice_multiply_fusion.2
  127.7 0.6 broadcast_in_dim.31
  128.3 8.5 %all-to-all-start.1 = ((f32[64,1,1]{2,1,0:T(1,128)}), f32[64,1,1]{2,1,0:T(1,128)S(1)}, u32[]{:S(2)}, u32[]{:S(2)}) async-start(f32[64,1,1]{2,1,0:T(1,128)} %broadcast_in_dim.31), calls=%async_computation.1 | async-start | bytes 65536 | tf_op jit(solution)/shard_map/all_to_all | solution.py:92
  136.9 0.1 copy.99
  137.0 0.1 copy.97
  137.2 0.1 copy.96
  137.4 7.1 %all-to-all-done.1 = f32[64,1,1]{2,1,0:T(1,128)S(1)} async-done(((f32[64,1,1]{2,1,0:T(1,128)}), f32[64,1,1]{2,1,0:T(1,128)S(1)}, u32[]{:S(2)}, u32[]{:S(2)}) %all-to-all-start.1) | async-done | bytes 288 | tf_op jit(solution)/shard_map/all_to_all | solution.py:92
  144.5 0.7 reduce_sum.49
  146.0 0.1 copy.98
  146.1 0.1 mul.249
  146.2 0.6 convert_bitcast_fusion.1
  146.9 0.7 convert_bitcast_fusion
  147.6 5.1 %broadcast_in_dim.32 = bf16[64,1,20768]{2,1,0:T(2,128)(2,1)} broadcast(bf16[20768]{0:T(1024)(128)(2,1)S(1)} %pad_maximum_fusion), dimensions={2} | broadcast | bytes 2699840 | tf_op jit(solution)/shard_map/broadcast_in_dim | solution.py:126
  152.7 55.7 %reduce.9 = bf16[64,20768]{1,0:T(8,128)(2,1)S(1)} reduce(bf16[64,1,20768]{2,1,0:T(2,128)(2,1)} %broadcast_in_dim.32, bf16[]{:T(256)} %broadcast.225), dimensions={1}, to_apply=%broadcast_in_dim.32.reduce_sub_computation | reduce | bytes 5316610 | tf_op jit(solution)/shard_map/broadcast_in_dim | solution.py:126
  208.4 4.0 %reshape.272 = bf16[64,2,10384]{2,1,0:T(2,128)(2,1)} reshape(bf16[64,20768]{1,0:T(8,128)(2,1)S(1)} %reduce.9) | data formatting | bytes 5316608
  212.4 6.7 %all-to-all-start.2 = ((bf16[64,2,10384]{2,1,0:T(2,128)(2,1)}), bf16[64,2,10384]{2,1,0:T(2,128)(2,1)S(1)}, u32[]{:S(2)}, u32[]{:S(2)}) async-start(bf16[64,2,10384]{2,1,0:T(2,128)(2,1)} %reshape.272), calls=%async_computation.2 | async-start | bytes 5373952 | tf_op jit(solution)/shard_map/all_to_all | solution.py:126
  219.2 0.6 constant_dynamic-slice_fusion.2
  219.7 0.6 constant_dynamic-slice_fusion
  220.3 59.6 %all-to-all-done.2 = bf16[64,2,10384]{2,1,0:T(2,128)(2,1)S(1)} async-done(((bf16[64,2,10384]{2,1,0:T(2,128)(2,1)}), bf16[64,2,10384]{2,1,0:T(2,128)(2,1)S(1)}, u32[]{:S(2)}, u32[]{:S(2)}) %all-to-all-start.2) | async-done | bytes 2658336 | tf_op jit(solution)/shard_map/all_to_all | solution.py:126
  279.9 8.0 %reshape.273 = bf16[64,1,20768]{2,1,0:T(2,128)(2,1)} reshape(bf16[64,2,10384]{2,1,0:T(2,128)(2,1)S(1)} %all-to-all-done.2) | data formatting | bytes 5316608
  287.9 13.3 %copy.101 = bf16[64,1,20768]{0,2,1:T(8,128)(2,1)} copy(bf16[64,1,20768]{2,1,0:T(2,128)(2,1)} %reshape.273) | data formatting | bytes 5316608 | tf_op jit(solution)/shard_map/all_to_all | solution.py:126
  301.2 0.9 slice_bitcast_fusion
  302.1 1.3 slice.68
  303.4 3.7 %slice.69 = bf16[64,16384]{0,1:T(8,128)(2,1)} slice(bf16[64,20768]{0,1:T(8,128)(2,1)} %bitcast.67), slice={[0:64], [4096:20480]} | slice | bytes 4194304 | tf_op jit(solution)/shard_map/slice | solution.py:129
  307.1 0.2 copy.105
  307.2 0.7 copy.106
  308.0 0.3 copy.102
  308.3 1.0 reshape.265
  309.4 5.6 %copy.104 = bf16[2,64,8,1024]{3,2,1,0:T(8,128)(2,1)} copy(bf16[2,64,8,1024]{1,3,2,0:T(8,128)(2,1)} %bitcast.68) | data formatting | bytes 4194304 | tf_op jit(solution)/shard_map/transpose | solution.py:131
  (44 shorter events, 0.9 us)
Async XLA Ops:
  15.8 72.8 %all-to-all-start = ((bf16[64,2,10384]{2,1,0:T(2,128)(2,1)}), bf16[64,2,10384]{2,1,0:T(2,128)(2,1)S(1)}, u32[]{:S(2)}, u32[]{:S(2)}) async-start(bf16[64,2,10384]{2,1,0:T(2,128)(2,1)} %reshape.270), calls=%async_computation | async-start | bytes 5373952 | tf_op jit(solution)/shard_map/all_to_all | solution.py:63
  96.7 11.0 %copy-start.6 = (f32[36,2]{0,1:T(2,128)S(1)}, f32[36,2]{0,1:T(2,128)}, u32[]{:S(2)}) copy-start(f32[36,2]{0,1:T(2,128)} %param.26) | copy-start | bytes 868
  96.7 11.1 %copy-start.7 = (f32[36,2]{0,1:T(2,128)S(1)}, f32[36,2]{0,1:T(2,128)}, u32[]{:S(2)}) copy-start(f32[36,2]{0,1:T(2,128)} %param.27) | copy-start | bytes 868
  96.7 11.2 %copy-start.8 = (f32[36,2]{0,1:T(2,128)S(1)}, f32[36,2]{0,1:T(2,128)}, u32[]{:S(2)}) copy-start(f32[36,2]{0,1:T(2,128)} %param.28) | copy-start | bytes 868
  96.7 49.5 %copy-start.3 = (f32[8,512]{1,0:T(8,128)S(1)}, f32[8,512]{1,0:T(8,128)}, u32[]{:S(2)}) copy-start(f32[8,512]{1,0:T(8,128)} %param.20) | copy-start | bytes 49156
  96.7 49.5 %copy-start.4 = (f32[8,512]{1,0:T(8,128)S(1)}, f32[8,512]{1,0:T(8,128)}, u32[]{:S(2)}) copy-start(f32[8,512]{1,0:T(8,128)} %param.22) | copy-start | bytes 49156
  96.7 49.5 %copy-start.5 = (f32[8,512]{1,0:T(8,128)S(1)}, f32[8,512]{1,0:T(8,128)}, u32[]{:S(2)}) copy-start(f32[8,512]{1,0:T(8,128)} %param.21) | copy-start | bytes 49156
  96.7 50.1 %copy-start = (f32[2,8,1024]{2,1,0:T(8,128)S(1)}, f32[2,8,1024]{2,1,0:T(8,128)}, u32[]{:S(2)}) copy-start(f32[2,8,1024]{2,1,0:T(8,128)} %param.23) | copy-start | bytes 196612
  96.8 50.1 %copy-start.1 = (f32[2,8,1024]{2,1,0:T(8,128)S(1)}, f32[2,8,1024]{2,1,0:T(8,128)}, u32[]{:S(2)}) copy-start(f32[2,8,1024]{2,1,0:T(8,128)} %param.25) | copy-start | bytes 196612
  96.8 50.1 %copy-start.2 = (f32[2,8,1024]{2,1,0:T(8,128)S(1)}, f32[2,8,1024]{2,1,0:T(8,128)}, u32[]{:S(2)}) copy-start(f32[2,8,1024]{2,1,0:T(8,128)} %param.24) | copy-start | bytes 196612
  128.3 16.2 %all-to-all-start.1 = ((f32[64,1,1]{2,1,0:T(1,128)}), f32[64,1,1]{2,1,0:T(1,128)S(1)}, u32[]{:S(2)}, u32[]{:S(2)}) async-start(f32[64,1,1]{2,1,0:T(1,128)} %broadcast_in_dim.31), calls=%async_computation.1 | async-start | bytes 65536 | tf_op jit(solution)/shard_map/all_to_all | solution.py:92
  212.4 67.5 %all-to-all-start.2 = ((bf16[64,2,10384]{2,1,0:T(2,128)(2,1)}), bf16[64,2,10384]{2,1,0:T(2,128)(2,1)S(1)}, u32[]{:S(2)}, u32[]{:S(2)}) async-start(bf16[64,2,10384]{2,1,0:T(2,128)(2,1)} %reshape.272), calls=%async_computation.2 | async-start | bytes 5373952 | tf_op jit(solution)/shard_map/all_to_all | solution.py:126

commit v2 on v1

--- a/solution.py
+++ b/solution.py
@@ -56,17 +56,12 @@
     rc = r_cols // n_dp
     own = rc // n_t
 
-    att_blocks = att.reshape(n_dp, ra * cols)
-    exp_blocks = exp.reshape(n_e, n_dp, re, e_cols).transpose(1, 0, 2, 3).reshape(n_dp, -1)
-    rte_blocks = rte.reshape(n_r, n_dp, rc).transpose(1, 0, 2).reshape(n_dp, -1)
-    send = jnp.concatenate([att_blocks, exp_blocks, rte_blocks], axis=1)
-    got = lax.all_to_all(send, "dp", 0, 0, tiled=True)
-    total = jnp.sum(got.astype(jnp.float32), axis=0)
-    n_att = ra * cols
-    n_exp = n_e * re * e_cols
-    attention_sum = total[:n_att].reshape(ra, cols)
-    expert_sum = total[n_att : n_att + n_exp].reshape(n_e, re, e_cols)
-    route_part = total[n_att + n_exp :].reshape(n_r, rc)
+    att_got = lax.all_to_all(att, "dp", 0, 0, tiled=True)
+    exp_got = lax.all_to_all(exp, "dp", 1, 1, tiled=True)
+    rte_got = lax.all_to_all(rte.T, "dp", 0, 0, tiled=True)
+    attention_sum = jnp.sum(att_got.reshape(n_dp, ra, cols).astype(jnp.float32), axis=0)
+    expert_sum = jnp.sum(exp_got.reshape(n_e, n_dp, re, e_cols).astype(jnp.float32), axis=1)
+    route_part = jnp.sum(rte_got.reshape(n_dp, rc, n_r).astype(jnp.float32), axis=0).T
 
     local_squares = jnp.sum(attention_sum * attention_sum) + jnp.sum(expert_sum * expert_sum)
     slot = (jnp.arange(rc) // own == t_idx)[None, :]
@@ -116,23 +111,20 @@
     def mine(values):
         return lax.dynamic_slice_in_dim(values, t_idx * own, own, axis=1)
 
-    served = jnp.concatenate(
-        [
-            attention_out[3].reshape(-1),
-            expert_out[3].reshape(-1),
-            routing_out[3].reshape(-1),
-        ]
+    att_srv = attention_out[3]
+    exp_srv = expert_out[3]
+    rte_srv = routing_out[3]
+    attention_served = lax.all_to_all(
+        jnp.broadcast_to(att_srv[None], (n_dp,) + att_srv.shape).reshape(rows, cols),
+        "dp", 0, 0, tiled=True,
     )
-    gathered = lax.all_to_all(jnp.broadcast_to(served, (n_dp,) + served.shape), "dp", 0, 0, tiled=True)
-    attention_served = gathered[:, :n_att].reshape(rows, cols)
-    expert_served = (
-        gathered[:, n_att : n_att + n_exp]
-        .reshape(n_dp, n_e, re, e_cols)
-        .transpose(1, 0, 2, 3)
-        .reshape(n_e, e_rows, e_cols)
+    expert_served = lax.all_to_all(
+        jnp.broadcast_to(exp_srv[:, None], (n_e, n_dp, re, e_cols)).reshape(n_e, e_rows, e_cols),
+        "dp", 1, 1, tiled=True,
     )
-    routing_served = (
-        gathered[:, n_att + n_exp :].reshape(n_dp, n_r, rc).transpose(1, 0, 2).reshape(n_r, r_cols)
+    routing_served = lax.all_to_all(
+        jnp.broadcast_to(rte_srv[:, None], (n_r, n_dp, rc)).reshape(n_r, r_cols),
+        "dp", 1, 1, tiled=True,
     )
     return (
         attention_out[0],

time: 320 us -> 247 us (0.77)
  other arithmetic: 71.7 us -> 5.99 us
  local copies, waits for them, and re-layouts: 67.2 us -> 17.3 us
  blocking collectives: 17.3 us -> 37.1 us
  starting transfers between devices: 27.4 us -> 41.5 us
  waiting for transfers between devices: 125 us -> 134 us
    broadcast_in_dim x1 -> x0, other arithmetic: 55.7 us -> none  [local(): jnp.broadcast_to(served, (n_dp,) + served.shape)]
    all_to_all x0 -> x1, blocking collectives: none -> 19.9 us  [local(): rte_got = lax.all_to_all(rte.T, 'dp', 0, 0, tiled=True)]
    unnamed x28, local copies, waits for them, and re-layouts: 28.6 us -> 9.82 us
    all_to_all x2 -> x5, starting transfers between devices: 18.8 us -> 33 us  [the longest x1 7.02 us: local(): exp_got = lax.all_to_all(exp, 'dp', 1, 1, tiled=True)]
    all_to_all x2 -> x1, local copies, waits for them, and re-layouts: 13.8 us -> 0.01 us  [local(): lax.all_to_all(jnp.broadcast_to(rte_srv[:, None], (n_r, n_dp, rc)).reshap...]
    all_to_all x2 -> x5, waiting for transfers between devices: 118 us -> 127 us  [the longest x1 46.6 us: local(): lax.all_to_all(jnp.broadcast_to(exp_srv[:, None], (n_e, n_dp, re, e_cols)...]
    transpose x4 -> x1, local copies, waits for them, and re-layouts: 6.88 us -> 0.93 us  [local(): rte_got = lax.all_to_all(rte.T, 'dp', 0, 0, tiled=True)]
    reduce_sum x1 -> x4, other arithmetic: 8.24 us -> 2.44 us  [the longest x1 1.67 us: local(): jnp.sum(exp_got.reshape(n_e, n_dp, re, e_cols).astype(jnp.float32), axis=1)]
  transfers between devices with their start and end apart: 3 -> 6, of which waited for: 3 -> 6; matrix products, arithmetic and copies ran while one was open for 1% -> 4% of each run, Pallas kernels for 0% -> 0%
where the time goes in v2:
time: 247 us; the launch traced here: 242 us
  waiting for transfers between devices  134 us (54%)
  starting transfers between devices  41.5 us (17%)
  blocking collectives  37.1 us (15%)
  local copies, waits for them, and re-layouts  17.3 us (7%)
  between operations  6.24 us (3%)
  other arithmetic  5.99 us (2%)
    all_to_all x1, waiting for transfers between devices, local(): lax.all_to_all(jnp.broadcast_to(exp_srv[:, None], (n_e, n_dp, re, e_cols)...  46.6 us
    all_to_all x1, waiting for transfers between devices, local(): exp_got = lax.all_to_all(exp, 'dp', 1, 1, tiled=True)  46.1 us
    all_to_all x1, blocking collectives, local(): rte_got = lax.all_to_all(rte.T, 'dp', 0, 0, tiled=True)  19.9 us
    psum x1, blocking collectives, local(): packed = lax.psum(packed, 'tensor')  17.2 us
    all_to_all x1, waiting for transfers between devices, local(): lax.all_to_all(jnp.broadcast_to(att_srv[None], (n_dp,) + att_srv.shape).r...  15.9 us
    all_to_all x1, waiting for transfers between devices, local(): att_got = lax.all_to_all(att, 'dp', 0, 0, tiled=True)  11.6 us
    unnamed x28, local copies, waits for them, and re-layouts  9.82 us
    all_to_all x1, starting transfers between devices, local(): squares = jnp.sum(lax.all_to_all(spread, 'dp', 0, 0, tiled=True))  8.44 us
  transfers between devices with their start and end apart: 6, of which 6 were waited for; matrix products, arithmetic and copies ran while one was open for 4% of the time, Pallas kernels for 0%

profile of v2, /device:TPU:4, one launch (start us, length us, event | category | flops | bytes accessed | tf_op | source)
XLA Modules:
  0.0 242.4 jit_solution(15073178980600171912)
XLA Ops:
  0.6 0.9 copy.69
  1.6 0.2 reshape.284
  1.7 19.9 %all_to_all.52 = bf16[64,2,144]{2,1,0:T(2,128)(2,1)S(1)} all-to-all(bf16[64,2,144]{2,1,0:T(2,128)(2,1)S(1)} %reshape.284), channel_id=1, replica_groups=mesh['dp'=64,'tensor'=4] {'dp'}, dimensions={0} | all-to-all | bytes 73728 | tf_op jit(solution)/shard_map/all_to_all | solution.py:61
  21.6 6.3 %all-to-all-start.1 = ((bf16[64,8,512]{2,1,0:T(8,128)(2,1)}), bf16[64,8,512]{2,1,0:T(8,128)(2,1)S(1)}, u32[]{:S(2)}, u32[]{:S(2)}) async-start(bf16[64,8,512]{2,1,0:T(8,128)(2,1)} %bitcast.60), calls=%async_computation.1 | async-start | bytes 1048576 | tf_op jit(solution)/shard_map/all_to_all | solution.py:59
  28.0 5.1 %copy.85 = bf16[1,1,2,512,1024]{4,2,3,1,0:T(2,128)(2,1)} copy(bf16[1,1,2,512,1024]{4,3,2,1,0:T(8,128)(2,1)} %param.18) | data formatting | bytes 4194304 | tf_op args[1]
  33.0 11.6 %all-to-all-done.1 = bf16[64,8,512]{2,1,0:T(8,128)(2,1)S(1)} async-done(((bf16[64,8,512]{2,1,0:T(8,128)(2,1)}), bf16[64,8,512]{2,1,0:T(8,128)(2,1)S(1)}, u32[]{:S(2)}, u32[]{:S(2)}) %all-to-all-start.1) | async-done | bytes 524320 | tf_op jit(solution)/shard_map/all_to_all | solution.py:59
  44.6 7.0 %all-to-all-start.2 = ((bf16[2,512,1024]{2,0,1:T(2,128)(2,1)}), bf16[2,512,1024]{2,0,1:T(2,128)(2,1)S(1)}, u32[]{:S(2)}, u32[]{:S(2)}) async-start(bf16[2,512,1024]{2,0,1:T(2,128)(2,1)} %bitcast.57), calls=%async_computation.2 | async-start | bytes 4194304 | tf_op jit(solution)/shard_map/all_to_all | solution.py:60
  51.7 0.0 copy-start.3
  51.7 0.0 copy-start.4
  51.7 0.0 copy-start.5
  53.1 0.1 reshape.285
  53.2 0.1 convert_reduce_fusion.2
  53.3 0.0 copy-done.6
  53.3 0.1 constant_dynamic-update-slice_fusion.3
  53.4 0.1 constant_dynamic-update-slice_fusion.2
  53.4 0.1 constant_dynamic-update-slice_fusion.1
  53.5 0.1 convert_reduce_fusion.1
  53.6 0.6 multiply_reduce_fusion.1
  54.2 46.1 %all-to-all-done.2 = bf16[2,512,1024]{2,0,1:T(2,128)(2,1)S(1)} async-done(((bf16[2,512,1024]{2,0,1:T(2,128)(2,1)}), bf16[2,512,1024]{2,0,1:T(2,128)(2,1)S(1)}, u32[]{:S(2)}, u32[]{:S(2)}) %all-to-all-start.2) | async-done | bytes 2097184 | tf_op jit(solution)/shard_map/all_to_all | solution.py:60
  100.3 1.7 convert_reduce_fusion
  101.9 0.7 multiply_reduce_fusion
  103.9 17.2 %psum.7 = f32[5,36,8]{1,2,0:T(8,128)S(1)} all-reduce(f32[5,36,8]{1,2,0:T(8,128)S(1)} %constant_dynamic-update-slice_fusion), channel_id=1, replica_groups=mesh['dp'=64,'tensor'=4] {'tensor'}, use_global_device_ids=true, to_apply=%region_5.6 | all-reduce | flops 1440 | bytes 11520 | tf_op jit(solution)/shard_map/psum | solution.py:81
  121.2 0.5 slice.36
  121.7 0.6 multiply_reduce_fusion.2
  123.6 0.6 broadcast_in_dim.46
  124.2 8.4 %all-to-all-start.3 = ((f32[64,1,1]{2,1,0:T(1,128)}), f32[64,1,1]{2,1,0:T(1,128)S(1)}, u32[]{:S(2)}, u32[]{:S(2)}) async-start(f32[64,1,1]{2,1,0:T(1,128)} %broadcast_in_dim.46), calls=%async_computation.3 | async-start | bytes 65536 | tf_op jit(solution)/shard_map/all_to_all | solution.py:87
  133.4 6.9 %all-to-all-done.3 = f32[64,1,1]{2,1,0:T(1,128)S(1)} async-done(((f32[64,1,1]{2,1,0:T(1,128)}), f32[64,1,1]{2,1,0:T(1,128)S(1)}, u32[]{:S(2)}, u32[]{:S(2)}) %all-to-all-start.3) | async-done | bytes 288 | tf_op jit(solution)/shard_map/all_to_all | solution.py:87
  140.3 0.7 reduce_sum.69
  141.8 0.8 reshape.286
  142.6 6.4 %all-to-all-start.6 = ((bf16[64,2,144]{2,1,0:T(2,128)(2,1)}), bf16[64,2,144]{2,1,0:T(2,128)(2,1)S(1)}, u32[]{:S(2)}, u32[]{:S(2)}) async-start(bf16[64,2,144]{2,1,0:T(2,128)(2,1)} %reshape.286), calls=%async_computation.6 | async-start | bytes 131072 | tf_op jit(solution)/shard_map/all_to_all | solution.py:125
  149.0 0.6 fusion.12
  149.7 7.3 %all-to-all-done.6 = bf16[64,2,144]{2,1,0:T(2,128)(2,1)S(1)} async-done(((bf16[64,2,144]{2,1,0:T(2,128)(2,1)}), bf16[64,2,144]{2,1,0:T(2,128)(2,1)S(1)}, u32[]{:S(2)}, u32[]{:S(2)}) %all-to-all-start.6) | async-done | bytes 36896 | tf_op jit(solution)/shard_map/all_to_all | solution.py:125
  157.0 0.8 broadcast_in_dim.47
  157.8 6.4 %all-to-all-start.4 = ((bf16[64,8,512]{2,1,0:T(8,128)(2,1)}), bf16[64,8,512]{2,1,0:T(8,128)(2,1)S(1)}, u32[]{:S(2)}, u32[]{:S(2)}) async-start(bf16[64,8,512]{2,1,0:T(8,128)(2,1)} %broadcast_in_dim.47), calls=%async_computation.4 | async-start | bytes 1048576 | tf_op jit(solution)/shard_map/all_to_all | solution.py:117
  164.2 0.0 copy-done
  164.2 0.0 copy-done.1
  164.2 0.0 copy-done.2
  164.2 0.7 fusion.10
  165.0 15.9 %all-to-all-done.4 = bf16[64,8,512]{2,1,0:T(8,128)(2,1)S(1)} async-done(((bf16[64,8,512]{2,1,0:T(8,128)(2,1)}), bf16[64,8,512]{2,1,0:T(8,128)(2,1)S(1)}, u32[]{:S(2)}, u32[]{:S(2)}) %all-to-all-start.4) | async-done | bytes 524320 | tf_op jit(solution)/shard_map/all_to_all | solution.py:117
  180.9 3.3 %broadcast_in_dim.48 = bf16[2,64,8,1024]{3,0,2,1:T(2,128)(2,1)} broadcast(bf16[2,8,1024]{2,0,1:T(2,128)(2,1)S(1)} %copy.73), dimensions={0,2,3} | broadcast | bytes 2129920 | tf_op jit(solution)/shard_map/broadcast_in_dim | solution.py:122
  184.2 6.9 %all-to-all-start.5 = ((bf16[2,512,1024]{2,0,1:T(2,128)(2,1)}), bf16[2,512,1024]{2,0,1:T(2,128)(2,1)S(1)}, u32[]{:S(2)}, u32[]{:S(2)}) async-start(bf16[2,512,1024]{2,0,1:T(2,128)(2,1)} %bitcast.58), calls=%async_computation.5 | async-start | bytes 4194304 | tf_op jit(solution)/shard_map/all_to_all | solution.py:121
  191.1 0.6 constant_dynamic-slice_fusion.2
  191.7 0.6 constant_dynamic-slice_fusion
  192.3 0.1 reshape.287
  192.4 0.7 copy.75
  193.1 46.6 %all-to-all-done.5 = bf16[2,512,1024]{2,0,1:T(2,128)(2,1)S(1)} async-done(((bf16[2,512,1024]{2,0,1:T(2,128)(2,1)}), bf16[2,512,1024]{2,0,1:T(2,128)(2,1)S(1)}, u32[]{:S(2)}, u32[]{:S(2)}) %all-to-all-start.5) | async-done | bytes 2097184 | tf_op jit(solution)/shard_map/all_to_all | solution.py:121
  239.7 1.9 copy.74
  241.7 0.8 copy.94
  (22 shorter events, 0.1 us)
Async XLA Ops:
  21.6 23.0 %all-to-all-start.1 = ((bf16[64,8,512]{2,1,0:T(8,128)(2,1)}), bf16[64,8,512]{2,1,0:T(8,128)(2,1)S(1)}, u32[]{:S(2)}, u32[]{:S(2)}) async-start(bf16[64,8,512]{2,1,0:T(8,128)(2,1)} %bitcast.60), calls=%async_computation.1 | async-start | bytes 1048576 | tf_op jit(solution)/shard_map/all_to_all | solution.py:59
  44.6 8.6 %copy-start.6 = (f32[36,2]{0,1:T(2,128)S(1)}, f32[36,2]{0,1:T(2,128)}, u32[]{:S(2)}) copy-start(f32[36,2]{0,1:T(2,128)} %param.26) | copy-start | bytes 868
  44.6 8.7 %copy-start.7 = (f32[36,2]{0,1:T(2,128)S(1)}, f32[36,2]{0,1:T(2,128)}, u32[]{:S(2)}) copy-start(f32[36,2]{0,1:T(2,128)} %param.27) | copy-start | bytes 868
  44.6 8.8 %copy-start.8 = (f32[36,2]{0,1:T(2,128)S(1)}, f32[36,2]{0,1:T(2,128)}, u32[]{:S(2)}) copy-start(f32[36,2]{0,1:T(2,128)} %param.28) | copy-start | bytes 868
  44.6 55.6 %all-to-all-start.2 = ((bf16[2,512,1024]{2,0,1:T(2,128)(2,1)}), bf16[2,512,1024]{2,0,1:T(2,128)(2,1)S(1)}, u32[]{:S(2)}, u32[]{:S(2)}) async-start(bf16[2,512,1024]{2,0,1:T(2,128)(2,1)} %bitcast.57), calls=%async_computation.2 | async-start | bytes 4194304 | tf_op jit(solution)/shard_map/all_to_all | solution.py:60
  51.7 97.3 %copy-start.3 = (f32[8,512]{1,0:T(8,128)S(1)}, f32[8,512]{1,0:T(8,128)}, u32[]{:S(2)}) copy-start(f32[8,512]{1,0:T(8,128)} %param.20) | copy-start | bytes 49156
  51.7 97.3 %copy-start.4 = (f32[8,512]{1,0:T(8,128)S(1)}, f32[8,512]{1,0:T(8,128)}, u32[]{:S(2)}) copy-start(f32[8,512]{1,0:T(8,128)} %param.22) | copy-start | bytes 49156
  51.7 97.3 %copy-start.5 = (f32[8,512]{1,0:T(8,128)S(1)}, f32[8,512]{1,0:T(8,128)}, u32[]{:S(2)}) copy-start(f32[8,512]{1,0:T(8,128)} %param.21) | copy-start | bytes 49156
  100.3 63.9 %copy-start = (f32[2,8,1024]{2,1,0:T(8,128)S(1)}, f32[2,8,1024]{2,1,0:T(8,128)}, u32[]{:S(2)}) copy-start(f32[2,8,1024]{2,1,0:T(8,128)} %param.23) | copy-start | bytes 196612
  100.3 63.9 %copy-start.1 = (f32[2,8,1024]{2,1,0:T(8,128)S(1)}, f32[2,8,1024]{2,1,0:T(8,128)}, u32[]{:S(2)}) copy-start(f32[2,8,1024]{2,1,0:T(8,128)} %param.25) | copy-start | bytes 196612
  100.3 64.0 %copy-start.2 = (f32[2,8,1024]{2,1,0:T(8,128)S(1)}, f32[2,8,1024]{2,1,0:T(8,128)}, u32[]{:S(2)}) copy-start(f32[2,8,1024]{2,1,0:T(8,128)} %param.24) | copy-start | bytes 196612
  124.2 16.1 %all-to-all-start.3 = ((f32[64,1,1]{2,1,0:T(1,128)}), f32[64,1,1]{2,1,0:T(1,128)S(1)}, u32[]{:S(2)}, u32[]{:S(2)}) async-start(f32[64,1,1]{2,1,0:T(1,128)} %broadcast_in_dim.46), calls=%async_computation.3 | async-start | bytes 65536 | tf_op jit(solution)/shard_map/all_to_all | solution.py:87
  142.6 14.4 %all-to-all-start.6 = ((bf16[64,2,144]{2,1,0:T(2,128)(2,1)}), bf16[64,2,144]{2,1,0:T(2,128)(2,1)S(1)}, u32[]{:S(2)}, u32[]{:S(2)}) async-start(bf16[64,2,144]{2,1,0:T(2,128)(2,1)} %reshape.286), calls=%async_computation.6 | async-start | bytes 131072 | tf_op jit(solution)/shard_map/all_to_all | solution.py:125
  157.8 23.1 %all-to-all-start.4 = ((bf16[64,8,512]{2,1,0:T(8,128)(2,1)}), bf16[64,8,512]{2,1,0:T(8,128)(2,1)S(1)}, u32[]{:S(2)}, u32[]{:S(2)}) async-start(bf16[64,8,512]{2,1,0:T(8,128)(2,1)} %broadcast_in_dim.47), calls=%async_computation.4 | async-start | bytes 1048576 | tf_op jit(solution)/shard_map/all_to_all | solution.py:117
  184.2 55.5 %all-to-all-start.5 = ((bf16[2,512,1024]{2,0,1:T(2,128)(2,1)}), bf16[2,512,1024]{2,0,1:T(2,128)(2,1)S(1)}, u32[]{:S(2)}, u32[]{:S(2)}) async-start(bf16[2,512,1024]{2,0,1:T(2,128)(2,1)} %bitcast.58), calls=%async_computation.5 | async-start | bytes 4194304 | tf_op jit(solution)/shard_map/all_to_all | solution.py:121

commit v3 on v2

--- a/solution.py
+++ b/solution.py
@@ -56,12 +56,13 @@
     rc = r_cols // n_dp
     own = rc // n_t
 
-    att_got = lax.all_to_all(att, "dp", 0, 0, tiled=True)
-    exp_got = lax.all_to_all(exp, "dp", 1, 1, tiled=True)
-    rte_got = lax.all_to_all(rte.T, "dp", 0, 0, tiled=True)
-    attention_sum = jnp.sum(att_got.reshape(n_dp, ra, cols).astype(jnp.float32), axis=0)
-    expert_sum = jnp.sum(exp_got.reshape(n_e, n_dp, re, e_cols).astype(jnp.float32), axis=1)
-    route_part = jnp.sum(rte_got.reshape(n_dp, rc, n_r).astype(jnp.float32), axis=0).T
+    exp_rows = exp.transpose(1, 0, 2).reshape(e_rows, n_e * e_cols)
+    send = jnp.concatenate([att, exp_rows, rte.T], axis=1)
+    got = lax.all_to_all(send, "dp", 0, 0, tiled=True)
+    total = jnp.sum(got.reshape(n_dp, ra, -1).astype(jnp.float32), axis=0)
+    attention_sum = total[:, :cols]
+    expert_sum = total[:, cols : cols + n_e * e_cols].reshape(re, n_e, e_cols).transpose(1, 0, 2)
+    route_part = total[:, cols + n_e * e_cols :].T
 
     local_squares = jnp.sum(attention_sum * attention_sum) + jnp.sum(expert_sum * expert_sum)
     slot = (jnp.arange(rc) // own == t_idx)[None, :]
@@ -111,21 +112,11 @@
     def mine(values):
         return lax.dynamic_slice_in_dim(values, t_idx * own, own, axis=1)
 
-    att_srv = attention_out[3]
-    exp_srv = expert_out[3]
-    rte_srv = routing_out[3]
-    attention_served = lax.all_to_all(
-        jnp.broadcast_to(att_srv[None], (n_dp,) + att_srv.shape).reshape(rows, cols),
-        "dp", 0, 0, tiled=True,
-    )
-    expert_served = lax.all_to_all(
-        jnp.broadcast_to(exp_srv[:, None], (n_e, n_dp, re, e_cols)).reshape(n_e, e_rows, e_cols),
-        "dp", 1, 1, tiled=True,
-    )
-    routing_served = lax.all_to_all(
-        jnp.broadcast_to(rte_srv[:, None], (n_r, n_dp, rc)).reshape(n_r, r_cols),
-        "dp", 1, 1, tiled=True,
-    )
+    rest = jnp.concatenate([attention_out[3], routing_out[3].T], axis=1)
+    rest = lax.all_gather(rest, "dp", axis=0, tiled=True)
+    expert_served = lax.all_gather(expert_out[3], "dp", axis=1, tiled=True)
+    attention_served = rest[:, :cols]
+    routing_served = rest[:, cols:].T
     return (
         attention_out[0],
         attention_out[1],

time: 247 us -> 218 us (0.88)
  waiting for transfers between devices: 134 us -> 86.7 us
  blocking collectives: 37.1 us -> 65.9 us
  starting transfers between devices: 41.5 us -> 20.6 us
  between operations: 6.24 us -> 19.7 us
    all_to_all x5 -> x1, waiting for transfers between devices: 127 us -> 60.6 us  [local(): got = lax.all_to_all(send, 'dp', 0, 0, tiled=True)]
    all_gather x0 -> x1, blocking collectives: none -> 48.6 us  [local(): rest = lax.all_gather(rest, 'dp', axis=0, tiled=True)]
    all_to_all x5 -> x1, starting transfers between devices: 33 us -> 12.1 us  [local(): got = lax.all_to_all(send, 'dp', 0, 0, tiled=True)]
    all_to_all x1 -> x0, blocking collectives: 19.9 us -> none  [local(): rte_got = lax.all_to_all(rte.T, 'dp', 0, 0, tiled=True)]
    all_gather x0 -> x1, waiting for transfers between devices: none -> 19.2 us  [local(): expert_served = lax.all_gather(expert_out[3], 'dp', axis=1, tiled=True)]
    unnamed x28 -> x25, local copies, waits for them, and re-layouts: 9.82 us -> 3.89 us
    transpose x1 -> x3, local copies, waits for them, and re-layouts: 0.93 us -> 5.22 us  [the longest x1 5.07 us: local(): exp_rows = exp.transpose(1, 0, 2).reshape(e_rows, n_e * e_cols)]
    broadcast_in_dim x2 -> x0, local copies, waits for them, and re-layouts: 4.17 us -> none  [the longest x1 3.34 us: local(): jnp.broadcast_to(exp_srv[:, None], (n_e, n_dp, re, e_cols))]
  transfers between devices with their start and end apart: 6 -> 3, of which waited for: 6 -> 3; matrix products, arithmetic and copies ran while one was open for 4% -> 2% of each run, Pallas kernels for 0% -> 0%
where the time goes in v3:
time: 218 us; the launch traced here: 215 us
  waiting for transfers between devices  86.7 us (40%)
  blocking collectives  65.9 us (30%)
  starting transfers between devices  20.6 us (9%)
  between operations  19.7 us (9%)
  local copies, waits for them, and re-layouts  15.6 us (7%)
  other arithmetic  6.41 us (3%)
    all_to_all x1, waiting for transfers between devices, local(): got = lax.all_to_all(send, 'dp', 0, 0, tiled=True)  60.6 us
    all_gather x1, blocking collectives, local(): rest = lax.all_gather(rest, 'dp', axis=0, tiled=True)  48.6 us
    all_gather x1, waiting for transfers between devices, local(): expert_served = lax.all_gather(expert_out[3], 'dp', axis=1, tiled=True)  19.2 us
    psum x1, blocking collectives, local(): packed = lax.psum(packed, 'tensor')  17.2 us
    all_to_all x1, starting transfers between devices, local(): got = lax.all_to_all(send, 'dp', 0, 0, tiled=True)  12.1 us
    all_to_all x1, starting transfers between devices, local(): squares = jnp.sum(lax.all_to_all(spread, 'dp', 0, 0, tiled=True))  8.49 us
    all_to_all x1, waiting for transfers between devices, local(): squares = jnp.sum(lax.all_to_all(spread, 'dp', 0, 0, tiled=True))  6.86 us
    transpose x1, local copies, waits for them, and re-layouts, local(): exp_rows = exp.transpose(1, 0, 2).reshape(e_rows, n_e * e_cols)  5.07 us
  transfers between devices with their start and end apart: 3, of which 3 were waited for; matrix products, arithmetic and copies ran while one was open for 2% of the time, Pallas kernels for 0%

profile of v3, /device:TPU:4, one launch (start us, length us, event | category | flops | bytes accessed | tf_op | source)
XLA Modules:
  0.0 214.9 jit_solution(13370848180475653956)
XLA Ops:
  7.2 5.1 %copy.54 = bf16[512,2,1024]{2,1,0:T(2,128)(2,1)} copy(bf16[512,2,1024]{2,0,1:T(8,128)(2,1)} %bitcast.55) | data formatting | bytes 4194304 | tf_op jit(solution)/shard_map/transpose | solution.py:59
  12.2 3.3 %concatenate.16 = bf16[64,8,2048]{2,1,0:T(8,128)(2,1)S(1)} reshape(bf16[512,2,1024]{2,1,0:T(2,128)(2,1)} %copy.54) | data formatting | bytes 4194304 | tf_op jit(solution)/shard_map/concatenate | solution.py:60
  15.6 0.0 copy-done.4
  15.6 0.1 copy.55
  15.8 0.0 copy-done
  15.8 1.8 pad_maximum_fusion
  17.5 12.1 %all-to-all-start = ((bf16[64,8,2596]{2,1,0:T(8,128)(2,1)}), bf16[64,8,2596]{2,1,0:T(8,128)(2,1)S(1)}, u32[]{:S(2)}, u32[]{:S(2)}) async-start(bf16[64,8,2596]{2,1,0:T(8,128)(2,1)} %pad_maximum_fusion), calls=%async_computation | async-start | bytes 5505024 | tf_op jit(solution)/shard_map/all_to_all | solution.py:61
  29.6 0.0 copy-start.8
  29.6 0.0 copy-start.9
  29.7 0.0 copy-start.10
  29.7 0.0 copy-start.1
  29.7 0.0 copy-start.2
  29.7 0.0 copy-start.3
  29.7 0.0 copy-start.5
  29.7 0.0 copy-start.6
  29.7 0.0 copy-start.7
  31.1 60.6 %all-to-all-done = bf16[64,8,2596]{2,1,0:T(8,128)(2,1)S(1)} async-done(((bf16[64,8,2596]{2,1,0:T(8,128)(2,1)}), bf16[64,8,2596]{2,1,0:T(8,128)(2,1)S(1)}, u32[]{:S(2)}, u32[]{:S(2)}) %all-to-all-start) | async-done | bytes 2658336 | tf_op jit(solution)/shard_map/all_to_all | solution.py:61
  91.8 0.5 convert_reduce_fusion
  92.3 0.6 multiply_reduce_fusion
  92.9 0.6 multiply_reduce_fusion.1
  93.5 0.0 copy-done.8
  93.6 0.1 constant_dynamic-update-slice_fusion.3
  93.6 0.0 copy-done.9
  93.6 0.1 constant_dynamic-update-slice_fusion.2
  93.7 0.0 copy-done.10
  93.7 0.1 constant_dynamic-update-slice_fusion.1
  95.1 17.2 %psum.7 = f32[5,36,8]{1,2,0:T(8,128)S(1)} all-reduce(f32[5,36,8]{1,2,0:T(8,128)S(1)} %constant_dynamic-update-slice_fusion), channel_id=1, replica_groups=mesh['dp'=64,'tensor'=4] {'tensor'}, use_global_device_ids=true, to_apply=%region_3.4 | all-reduce | flops 1440 | bytes 11520 | tf_op jit(solution)/shard_map/psum | solution.py:82
  112.3 0.5 slice.59
  112.9 0.6 multiply_reduce_fusion.2
  114.8 0.6 broadcast_in_dim.28
  115.4 8.5 %all-to-all-start.1 = ((f32[64,1,1]{2,1,0:T(1,128)}), f32[64,1,1]{2,1,0:T(1,128)S(1)}, u32[]{:S(2)}, u32[]{:S(2)}) async-start(f32[64,1,1]{2,1,0:T(1,128)} %broadcast_in_dim.28), calls=%async_computation.1 | async-start | bytes 65536 | tf_op jit(solution)/shard_map/all_to_all | solution.py:88
  123.9 0.0 all-gather.2.cloned.1.call-start
  124.7 6.9 %all-to-all-done.1 = f32[64,1,1]{2,1,0:T(1,128)S(1)} async-done(((f32[64,1,1]{2,1,0:T(1,128)}), f32[64,1,1]{2,1,0:T(1,128)S(1)}, u32[]{:S(2)}, u32[]{:S(2)}) %all-to-all-start.1) | async-done | bytes 288 | tf_op jit(solution)/shard_map/all_to_all | solution.py:88
  131.5 0.7 reduce_sum.49
  133.0 0.0 copy-done.1
  133.0 0.0 copy-done.2
  133.0 0.0 copy-done.3
  133.0 0.7 fusion.7
  133.7 0.0 all-gather.2.cloned.1.call-update
  133.7 0.0 copy-done.5
  133.8 0.6 fusion.9
  134.4 48.6 %all_gather.6 = bf16[512,548]{1,0:T(8,128)(2,1)S(1)} all-gather(bf16[8,548]{1,0:T(8,128)(2,1)S(1)} %pad_maximum_fusion.1), channel_id=1, replica_groups=mesh['dp'=64,'tensor'=4] {'dp'}, dimensions={0}, use_global_device_ids=true | all-gather | bytes 569920 | tf_op jit(solution)/shard_map/all_gather | solution.py:116
  183.0 0.8 slice.64
  183.9 0.7 copy.57
  184.6 0.6 constant_dynamic-slice_fusion.2
  185.2 0.6 constant_dynamic-slice_fusion
  185.8 19.2 %all-gather.2.cloned.1.call-done = bf16[2,512,1024]{2,1,0:T(8,128)(2,1)} async-done(((bf16[2,8,1024]{2,1,0:T(8,128)(2,1)}), bf16[2,512,1024]{2,1,0:T(8,128)(2,1)}) %all-gather.2.cloned.1.call-update) | async-done | bytes 2097168 | tf_op jit(solution)/shard_map/all_gather | solution.py:117
  204.9 3.1 %copy.67 = bf16[2,512,1024]{2,1,0:T(8,128)(2,1)} copy(bf16[2,512,1024]{2,1,0:T(8,128)(2,1)} %all-gather.2.cloned.1.call-done) | data formatting | bytes 4194304
  (15 shorter events, 0.1 us)
Async XLA Ops:
  12.2 3.4 %copy-start.4 = (bf16[1,1,1,36,512]{4,3,2,1,0:T(8,128)(2,1)S(1)}, bf16[1,1,1,36,512]{4,3,2,1,0:T(8,128)(2,1)}, u32[]{:S(2)}) copy-start(bf16[1,1,1,36,512]{4,3,2,1,0:T(8,128)(2,1)} %param.19) | copy-start | bytes 110596
  12.2 3.5 %copy-start = (bf16[1,1,512,512]{3,2,1,0:T(8,128)(2,1)S(1)}, bf16[1,1,512,512]{3,2,1,0:T(8,128)(2,1)}, u32[]{:S(2)}) copy-start(bf16[1,1,512,512]{3,2,1,0:T(8,128)(2,1)} %param.17) | copy-start | bytes 1572868
  17.5 74.2 %all-to-all-start = ((bf16[64,8,2596]{2,1,0:T(8,128)(2,1)}), bf16[64,8,2596]{2,1,0:T(8,128)(2,1)S(1)}, u32[]{:S(2)}, u32[]{:S(2)}) async-start(bf16[64,8,2596]{2,1,0:T(8,128)(2,1)} %pad_maximum_fusion), calls=%async_computation | async-start | bytes 5505024 | tf_op jit(solution)/shard_map/all_to_all | solution.py:61
  29.6 63.9 %copy-start.8 = (f32[36,2]{0,1:T(2,128)S(1)}, f32[36,2]{0,1:T(2,128)}, u32[]{:S(2)}) copy-start(f32[36,2]{0,1:T(2,128)} %param.26) | copy-start | bytes 868
  29.6 64.0 %copy-start.9 = (f32[36,2]{0,1:T(2,128)S(1)}, f32[36,2]{0,1:T(2,128)}, u32[]{:S(2)}) copy-start(f32[36,2]{0,1:T(2,128)} %param.27) | copy-start | bytes 868
  29.7 64.0 %copy-start.10 = (f32[36,2]{0,1:T(2,128)S(1)}, f32[36,2]{0,1:T(2,128)}, u32[]{:S(2)}) copy-start(f32[36,2]{0,1:T(2,128)} %param.28) | copy-start | bytes 868
  29.7 103.3 %copy-start.1 = (f32[2,8,1024]{2,1,0:T(8,128)S(1)}, f32[2,8,1024]{2,1,0:T(8,128)}, u32[]{:S(2)}) copy-start(f32[2,8,1024]{2,1,0:T(8,128)} %param.23) | copy-start | bytes 196612
  29.7 103.3 %copy-start.2 = (f32[2,8,1024]{2,1,0:T(8,128)S(1)}, f32[2,8,1024]{2,1,0:T(8,128)}, u32[]{:S(2)}) copy-start(f32[2,8,1024]{2,1,0:T(8,128)} %param.25) | copy-start | bytes 196612
  29.7 103.3 %copy-start.3 = (f32[2,8,1024]{2,1,0:T(8,128)S(1)}, f32[2,8,1024]{2,1,0:T(8,128)}, u32[]{:S(2)}) copy-start(f32[2,8,1024]{2,1,0:T(8,128)} %param.24) | copy-start | bytes 196612
  29.7 104.0 %copy-start.5 = (f32[8,512]{1,0:T(8,128)S(1)}, f32[8,512]{1,0:T(8,128)}, u32[]{:S(2)}) copy-start(f32[8,512]{1,0:T(8,128)} %param.20) | copy-start | bytes 49156
  29.7 104.0 %copy-start.6 = (f32[8,512]{1,0:T(8,128)S(1)}, f32[8,512]{1,0:T(8,128)}, u32[]{:S(2)}) copy-start(f32[8,512]{1,0:T(8,128)} %param.22) | copy-start | bytes 49156
  29.7 104.0 %copy-start.7 = (f32[8,512]{1,0:T(8,128)S(1)}, f32[8,512]{1,0:T(8,128)}, u32[]{:S(2)}) copy-start(f32[8,512]{1,0:T(8,128)} %param.21) | copy-start | bytes 49156
  115.4 16.1 %all-to-all-start.1 = ((f32[64,1,1]{2,1,0:T(1,128)}), f32[64,1,1]{2,1,0:T(1,128)S(1)}, u32[]{:S(2)}, u32[]{:S(2)}) async-start(f32[64,1,1]{2,1,0:T(1,128)} %broadcast_in_dim.28), calls=%async_computation.1 | async-start | bytes 65536 | tf_op jit(solution)/shard_map/all_to_all | solution.py:88
  123.9 81.1 %all-gather.2.cloned.1.call-start = ((), (), s32[]{:S(2)}) async-start(), calls=%async_computation.2 | async-start | bytes 2129920 | tf_op jit(solution)/shard_map/all_gather | solution.py:117
Sparse Core Ops, SparseCore 0:
  133.8 71.0 all-gather.1

commit v4 on v3

--- a/solution.py
+++ b/solution.py
@@ -1,7 +1,7 @@
 import jax
 import jax.numpy as jnp
 from jax import lax
-from jax.sharding import PartitionSpec as P
+from jax.sharding import Mesh, PartitionSpec as P
 
 EXPERTS = 32
 PARAMS = 5261312
@@ -11,6 +11,9 @@
 BETA_TWO = 0.999
 EPSILON = 1e-08
 DECAY = 0.1
+
+DP_PARTS = ("dp_x", "dp_z", "dp_core")
+DP = DP_PARTS
 
 
 def adam_update(grad_sum, master, first, second, clip, rate, first_fix, second_fix, mask):
@@ -41,7 +44,7 @@
     learn_rate,
     clip_level,
 ):
-    n_dp = lax.axis_size("dp")
+    n_dp = lax.axis_size(DP)
     n_t = lax.axis_size("tensor")
     t_idx = lax.axis_index("tensor")
 
@@ -58,7 +61,7 @@
 
     exp_rows = exp.transpose(1, 0, 2).reshape(e_rows, n_e * e_cols)
     send = jnp.concatenate([att, exp_rows, rte.T], axis=1)
-    got = lax.all_to_all(send, "dp", 0, 0, tiled=True)
+    got = lax.all_to_all(send, DP, 0, 0, tiled=True)
     total = jnp.sum(got.reshape(n_dp, ra, -1).astype(jnp.float32), axis=0)
     attention_sum = total[:, :cols]
     expert_sum = total[:, cols : cols + n_e * e_cols].reshape(re, n_e, e_cols).transpose(1, 0, 2)
@@ -85,7 +88,7 @@
     group_squares = packed[4, 0, 0] + jnp.sum(route_sum * route_sum)
 
     spread = jnp.broadcast_to(group_squares, (n_dp, 1))
-    squares = jnp.sum(lax.all_to_all(spread, "dp", 0, 0, tiled=True))
+    squares = jnp.sum(lax.all_to_all(spread, DP, 0, 0, tiled=True))
 
     grad_norm = jnp.sqrt(squares)
     clip = jnp.minimum(1.0, clip_level[0] * jnp.sqrt(jnp.float32(PARAMS)) / (grad_norm + 1e-06))
@@ -112,9 +115,13 @@
     def mine(values):
         return lax.dynamic_slice_in_dim(values, t_idx * own, own, axis=1)
 
-    rest = jnp.concatenate([attention_out[3], routing_out[3].T], axis=1)
-    rest = lax.all_gather(rest, "dp", axis=0, tiled=True)
-    expert_served = lax.all_gather(expert_out[3], "dp", axis=1, tiled=True)
+    def gather(values, axis):
+        for name in reversed(DP_PARTS):
+            values = lax.all_gather(values, name, axis=axis, tiled=True)
+        return values
+
+    rest = gather(jnp.concatenate([attention_out[3], routing_out[3].T], axis=1), 0)
+    expert_served = gather(expert_out[3], 1)
     attention_served = rest[:, :cols]
     routing_served = rest[:, cols:].T
     return (
@@ -133,36 +140,48 @@
     )
 
 
+def split_mesh(mesh):
+    column = mesh.devices[:, 0]
+    sizes = (
+        len({d.coords[0] for d in column}),
+        len({d.coords[2] for d in column}),
+        len({d.core_on_chip for d in column}),
+    )
+    devices = mesh.devices.reshape(sizes + mesh.devices.shape[1:])
+    return Mesh(devices, DP_PARTS + ("tensor",))
+
+
 def solution(mesh):
+    mesh = split_mesh(mesh)
     in_specs = (
-        P("dp", None, None, "tensor"),
-        P("dp", None, None, None, "tensor"),
-        P("dp", "tensor", None, None, None),
-        P("dp", "tensor"),
-        P("dp", "tensor"),
-        P("dp", "tensor"),
-        P(None, "dp", "tensor"),
-        P(None, "dp", "tensor"),
-        P(None, "dp", "tensor"),
-        P(None, ("dp", "tensor")),
-        P(None, ("dp", "tensor")),
-        P(None, ("dp", "tensor")),
+        P(DP, None, None, "tensor"),
+        P(DP, None, None, None, "tensor"),
+        P(DP, "tensor", None, None, None),
+        P(DP, "tensor"),
+        P(DP, "tensor"),
+        P(DP, "tensor"),
+        P(None, DP, "tensor"),
+        P(None, DP, "tensor"),
+        P(None, DP, "tensor"),
+        P(None, (DP + ("tensor",))),
+        P(None, (DP + ("tensor",))),
+        P(None, (DP + ("tensor",))),
         P(),
         P(),
         P(),
     )
     out_specs = (
-        P("dp", "tensor"),
-        P("dp", "tensor"),
-        P("dp", "tensor"),
+        P(DP, "tensor"),
+        P(DP, "tensor"),
+        P(DP, "tensor"),
         P(None, "tensor"),
-        P(None, "dp", "tensor"),
-        P(None, "dp", "tensor"),
-        P(None, "dp", "tensor"),
+        P(None, DP, "tensor"),
+        P(None, DP, "tensor"),
+        P(None, DP, "tensor"),
         P(None, None, "tensor"),
-        P(None, ("dp", "tensor")),
-        P(None, ("dp", "tensor")),
-        P(None, ("dp", "tensor")),
+        P(None, (DP + ("tensor",))),
+        P(None, (DP + ("tensor",))),
+        P(None, (DP + ("tensor",))),
         P(),
     )
     return jax.shard_map(local, mesh=mesh, in_specs=in_specs, out_specs=out_specs, check_vma=False)

time: 218 us -> 217 us (level); the launches traced: 215 us -> 217 us
  blocking collectives: 65.9 us -> 87 us
  waiting for transfers between devices: 86.7 us -> 67.5 us
    all_gather x1 -> x5, blocking collectives: 48.6 us -> 69.7 us  [gather(): values = lax.all_gather(values, name, axis=axis, tiled=True)]
    all_gather x1, waiting for transfers between devices: 19.2 us -> 0.01 us  [gather(): values = lax.all_gather(values, name, axis=axis, tiled=True)]
  transfers between devices with their start and end apart: 3 -> 3, of which waited for: 3 -> 2; matrix products, arithmetic and copies ran while one was open for 2% -> 2% of each run, Pallas kernels for 0% -> 0%
where the time goes in v4:
time: 217 us
  blocking collectives  87 us (40%)
  waiting for transfers between devices  67.5 us (31%)
  starting transfers between devices  20.6 us (9%)
  between operations  19.7 us (9%)
  local copies, waits for them, and re-layouts  15.6 us (7%)
  other arithmetic  6.4 us (3%)
    all_gather x5, blocking collectives, gather(): values = lax.all_gather(values, name, axis=axis, tiled=True)  69.7 us
    all_to_all x1, waiting for transfers between devices, local(): got = lax.all_to_all(send, DP, 0, 0, tiled=True)  60.6 us
    psum x1, blocking collectives, local(): packed = lax.psum(packed, 'tensor')  17.2 us
    all_to_all x1, starting transfers between devices, local(): got = lax.all_to_all(send, DP, 0, 0, tiled=True)  12.1 us
    all_to_all x1, starting transfers between devices, local(): squares = jnp.sum(lax.all_to_all(spread, DP, 0, 0, tiled=True))  8.49 us
    all_to_all x1, waiting for transfers between devices, local(): squares = jnp.sum(lax.all_to_all(spread, DP, 0, 0, tiled=True))  6.86 us
    transpose x1, local copies, waits for them, and re-layouts, local(): exp_rows = exp.transpose(1, 0, 2).reshape(e_rows, n_e * e_cols)  5.07 us
  transfers between devices with their start and end apart: 3, of which 2 were waited for; matrix products, arithmetic and copies ran while one was open for 2% of the time, Pallas kernels for 0%

profile of v4, /device:TPU:4, one launch (start us, length us, event | category | flops | bytes accessed | tf_op | source)
XLA Modules:
  0.0 216.8 jit_solution(14723467126513611588)
XLA Ops:
  7.2 5.1 %copy.54 = bf16[512,2,1024]{2,1,0:T(2,128)(2,1)} copy(bf16[512,2,1024]{2,0,1:T(8,128)(2,1)} %bitcast.55) | data formatting | bytes 4194304 | tf_op jit(solution)/shard_map/transpose | solution.py:62
  12.2 3.3 %concatenate.16 = bf16[64,8,2048]{2,1,0:T(8,128)(2,1)S(1)} reshape(bf16[512,2,1024]{2,1,0:T(2,128)(2,1)} %copy.54) | data formatting | bytes 4194304 | tf_op jit(solution)/shard_map/concatenate | solution.py:63
  15.6 0.0 copy-done.4
  15.6 0.1 copy.55
  15.8 0.0 copy-done
  15.8 1.8 pad_maximum_fusion
  17.5 12.1 %all-to-all-start = ((bf16[64,8,2596]{2,1,0:T(8,128)(2,1)}), bf16[64,8,2596]{2,1,0:T(8,128)(2,1)S(1)}, u32[]{:S(2)}, u32[]{:S(2)}) async-start(bf16[64,8,2596]{2,1,0:T(8,128)(2,1)} %pad_maximum_fusion), calls=%async_computation | async-start | bytes 5505024 | tf_op jit(solution)/shard_map/all_to_all | solution.py:64
  29.6 0.0 copy-start.8
  29.6 0.0 copy-start.9
  29.7 0.0 copy-start.10
  29.7 0.0 copy-start.1
  29.7 0.0 copy-start.2
  29.7 0.0 copy-start.3
  29.7 0.0 copy-start.5
  29.7 0.0 copy-start.6
  29.7 0.0 copy-start.7
  31.1 60.6 %all-to-all-done = bf16[64,8,2596]{2,1,0:T(8,128)(2,1)S(1)} async-done(((bf16[64,8,2596]{2,1,0:T(8,128)(2,1)}), bf16[64,8,2596]{2,1,0:T(8,128)(2,1)S(1)}, u32[]{:S(2)}, u32[]{:S(2)}) %all-to-all-start) | async-done | bytes 2658336 | tf_op jit(solution)/shard_map/all_to_all | solution.py:64
  91.8 0.5 convert_reduce_fusion
  92.3 0.6 multiply_reduce_fusion
  92.9 0.6 multiply_reduce_fusion.1
  93.5 0.0 copy-done.8
  93.6 0.1 constant_dynamic-update-slice_fusion.3
  93.6 0.0 copy-done.9
  93.6 0.1 constant_dynamic-update-slice_fusion.2
  93.7 0.0 copy-done.10
  93.7 0.1 constant_dynamic-update-slice_fusion.1
  95.1 17.2 %psum.7 = f32[5,36,8]{1,2,0:T(8,128)S(1)} all-reduce(f32[5,36,8]{1,2,0:T(8,128)S(1)} %constant_dynamic-update-slice_fusion), channel_id=1, replica_groups=mesh['dp_x'=4,'dp_z'=8,'dp_core'=2,'tensor'=4] {'tensor'}, use_global_device_ids=true, to_apply=%region_3.4 | all-reduce | flops 1440 | bytes 11520 | tf_op jit(solution)/shard_map/psum | solution.py:85
  112.3 0.5 slice.59
  112.9 0.6 multiply_reduce_fusion.2
  114.8 0.6 broadcast_in_dim.28
  115.4 8.5 %all-to-all-start.1 = ((f32[64,1,1]{2,1,0:T(1,128)}), f32[64,1,1]{2,1,0:T(1,128)S(1)}, u32[]{:S(2)}, u32[]{:S(2)}) async-start(f32[64,1,1]{2,1,0:T(1,128)} %broadcast_in_dim.28), calls=%async_computation.1 | async-start | bytes 65536 | tf_op jit(solution)/shard_map/all_to_all | solution.py:91
  123.9 0.0 all-gather.2.cloned.1.call-start
  124.7 6.9 %all-to-all-done.1 = f32[64,1,1]{2,1,0:T(1,128)S(1)} async-done(((f32[64,1,1]{2,1,0:T(1,128)}), f32[64,1,1]{2,1,0:T(1,128)S(1)}, u32[]{:S(2)}, u32[]{:S(2)}) %all-to-all-start.1) | async-done | bytes 288 | tf_op jit(solution)/shard_map/all_to_all | solution.py:91
  131.5 0.7 reduce_sum.49
  133.0 0.0 copy-done.1
  133.0 0.7 fusion.7
  133.7 1.8 all_gather.21
  135.5 27.5 %all_gather.22 = bf16[2,128,1024]{2,1,0:T(8,128)(2,1)} all-gather(bf16[2,16,1024]{2,1,0:T(8,128)(2,1)S(1)} %all_gather.21), channel_id=1, replica_groups=mesh['dp_x'=4,'dp_z'=8,'dp_core'=2,'tensor'=4] {'dp_z'}, dimensions={1}, use_global_device_ids=true | all-gather | bytes 589824 | tf_op jit(solution)/shard_map/all_gather | solution.py:120
  163.0 0.0 all-gather.2.cloned.1.call-update
  163.1 0.6 fusion.9
  163.8 1.8 all_gather.18
  165.6 24.6 %all_gather.19 = bf16[128,548]{1,0:T(8,128)(2,1)S(1)} all-gather(bf16[16,548]{1,0:T(8,128)(2,1)S(1)} %all_gather.18), channel_id=1, replica_groups=mesh['dp_x'=4,'dp_z'=8,'dp_core'=2,'tensor'=4] {'dp_z'}, dimensions={0}, use_global_device_ids=true | all-gather | bytes 157824 | tf_op jit(solution)/shard_map/all_gather | solution.py:120
  190.2 13.9 %all_gather.20 = bf16[512,548]{1,0:T(8,128)(2,1)S(1)} all-gather(bf16[128,548]{1,0:T(8,128)(2,1)S(1)} %all_gather.19), channel_id=1, replica_groups=mesh['dp_x'=4,'dp_z'=8,'dp_core'=2,'tensor'=4] {'dp_x'}, dimensions={0}, use_global_device_ids=true | all-gather | bytes 701440 | tf_op jit(solution)/shard_map/all_gather | solution.py:120
  204.2 0.8 slice.64
  205.0 0.7 copy.57
  205.7 0.6 constant_dynamic-slice_fusion.2
  206.3 0.6 constant_dynamic-slice_fusion
  206.9 3.1 %copy.67 = bf16[2,512,1024]{2,1,0:T(8,128)(2,1)} copy(bf16[2,512,1024]{2,1,0:T(8,128)(2,1)} %all-gather.2.cloned.1.call-done) | data formatting | bytes 4194304
  (19 shorter events, 0.1 us)
Async XLA Ops:
  12.2 3.4 %copy-start.4 = (bf16[1,1,1,36,512]{4,3,2,1,0:T(8,128)(2,1)S(1)}, bf16[1,1,1,36,512]{4,3,2,1,0:T(8,128)(2,1)}, u32[]{:S(2)}) copy-start(bf16[1,1,1,36,512]{4,3,2,1,0:T(8,128)(2,1)} %param.19) | copy-start | bytes 110596
  12.2 3.5 %copy-start = (bf16[1,1,512,512]{3,2,1,0:T(8,128)(2,1)S(1)}, bf16[1,1,512,512]{3,2,1,0:T(8,128)(2,1)}, u32[]{:S(2)}) copy-start(bf16[1,1,512,512]{3,2,1,0:T(8,128)(2,1)} %param.17) | copy-start | bytes 1572868
  17.5 74.2 %all-to-all-start = ((bf16[64,8,2596]{2,1,0:T(8,128)(2,1)}), bf16[64,8,2596]{2,1,0:T(8,128)(2,1)S(1)}, u32[]{:S(2)}, u32[]{:S(2)}) async-start(bf16[64,8,2596]{2,1,0:T(8,128)(2,1)} %pad_maximum_fusion), calls=%async_computation | async-start | bytes 5505024 | tf_op jit(solution)/shard_map/all_to_all | solution.py:64
  29.6 63.9 %copy-start.8 = (f32[36,2]{0,1:T(2,128)S(1)}, f32[36,2]{0,1:T(2,128)}, u32[]{:S(2)}) copy-start(f32[36,2]{0,1:T(2,128)} %param.26) | copy-start | bytes 868
  29.6 64.0 %copy-start.9 = (f32[36,2]{0,1:T(2,128)S(1)}, f32[36,2]{0,1:T(2,128)}, u32[]{:S(2)}) copy-start(f32[36,2]{0,1:T(2,128)} %param.27) | copy-start | bytes 868
  29.7 64.0 %copy-start.10 = (f32[36,2]{0,1:T(2,128)S(1)}, f32[36,2]{0,1:T(2,128)}, u32[]{:S(2)}) copy-start(f32[36,2]{0,1:T(2,128)} %param.28) | copy-start | bytes 868
  29.7 103.3 %copy-start.1 = (f32[2,8,1024]{2,1,0:T(8,128)S(1)}, f32[2,8,1024]{2,1,0:T(8,128)}, u32[]{:S(2)}) copy-start(f32[2,8,1024]{2,1,0:T(8,128)} %param.23) | copy-start | bytes 196612
  29.7 103.3 %copy-start.2 = (f32[2,8,1024]{2,1,0:T(8,128)S(1)}, f32[2,8,1024]{2,1,0:T(8,128)}, u32[]{:S(2)}) copy-start(f32[2,8,1024]{2,1,0:T(8,128)} %param.25) | copy-start | bytes 196612
  29.7 103.3 %copy-start.3 = (f32[2,8,1024]{2,1,0:T(8,128)S(1)}, f32[2,8,1024]{2,1,0:T(8,128)}, u32[]{:S(2)}) copy-start(f32[2,8,1024]{2,1,0:T(8,128)} %param.24) | copy-start | bytes 196612
  29.7 133.4 %copy-start.5 = (f32[8,512]{1,0:T(8,128)S(1)}, f32[8,512]{1,0:T(8,128)}, u32[]{:S(2)}) copy-start(f32[8,512]{1,0:T(8,128)} %param.20) | copy-start | bytes 49156
  29.7 133.4 %copy-start.6 = (f32[8,512]{1,0:T(8,128)S(1)}, f32[8,512]{1,0:T(8,128)}, u32[]{:S(2)}) copy-start(f32[8,512]{1,0:T(8,128)} %param.22) | copy-start | bytes 49156
  29.7 133.4 %copy-start.7 = (f32[8,512]{1,0:T(8,128)S(1)}, f32[8,512]{1,0:T(8,128)}, u32[]{:S(2)}) copy-start(f32[8,512]{1,0:T(8,128)} %param.21) | copy-start | bytes 49156
  115.4 16.1 %all-to-all-start.1 = ((f32[64,1,1]{2,1,0:T(1,128)}), f32[64,1,1]{2,1,0:T(1,128)S(1)}, u32[]{:S(2)}, u32[]{:S(2)}) async-start(f32[64,1,1]{2,1,0:T(1,128)} %broadcast_in_dim.28), calls=%async_computation.1 | async-start | bytes 65536 | tf_op jit(solution)/shard_map/all_to_all | solution.py:91
  123.9 83.0 %all-gather.2.cloned.1.call-start = ((), (), s32[]{:S(2)}) async-start(), calls=%async_computation.2 | async-start | bytes 2621440 | tf_op jit(solution)/shard_map/all_gather | solution.py:120
Sparse Core Ops, SparseCore 0:
  163.2 27.5 all-gather.1

commit v5 on v4

--- a/solution.py
+++ b/solution.py
@@ -120,10 +120,20 @@
             values = lax.all_gather(values, name, axis=axis, tiled=True)
         return values
 
-    rest = gather(jnp.concatenate([attention_out[3], routing_out[3].T], axis=1), 0)
-    expert_served = gather(expert_out[3], 1)
+    rest = jnp.concatenate(
+        [
+            attention_out[3],
+            expert_out[3].transpose(1, 0, 2).reshape(re, n_e * e_cols),
+            routing_out[3].T,
+        ],
+        axis=1,
+    )
+    rest = gather(rest, 0)
     attention_served = rest[:, :cols]
-    routing_served = rest[:, cols:].T
+    expert_served = (
+        rest[:, cols : cols + n_e * e_cols].reshape(e_rows, n_e, e_cols).transpose(1, 0, 2)
+    )
+    routing_served = rest[:, cols + n_e * e_cols :].T
     return (
         attention_out[0],
         attention_out[1],

time: 217 us -> 213 us (0.982); the launches traced: 217 us -> 210 us
  blocking collectives: 87 us -> 47 us
  waiting for transfers between devices: 67.5 us -> 99.7 us
    all_gather x5 -> x2, blocking collectives: 69.7 us -> 29.7 us  [gather(): values = lax.all_gather(values, name, axis=axis, tiled=True)]
    all_gather x1, waiting for transfers between devices: 0.01 us -> 32.2 us  [gather(): values = lax.all_gather(values, name, axis=axis, tiled=True)]
  transfers between devices with their start and end apart: 3 -> 3, of which waited for: 2 -> 3; matrix products, arithmetic and copies ran while one was open for 2% -> 1% of each run, Pallas kernels for 0% -> 0%
where the time goes in v5:
time: 213 us; the launch traced here: 210 us
  waiting for transfers between devices  99.7 us (47%)
  blocking collectives  47 us (22%)
  starting transfers between devices  20.6 us (10%)
  between operations  19.7 us (9%)
  local copies, waits for them, and re-layouts  16.9 us (8%)
  other arithmetic  6.39 us (3%)
    all_to_all x1, waiting for transfers between devices, local(): got = lax.all_to_all(send, DP, 0, 0, tiled=True)  60 us
    all_gather x1, waiting for transfers between devices, gather(): values = lax.all_gather(values, name, axis=axis, tiled=True)  32.2 us
    all_gather x2, blocking collectives, gather(): values = lax.all_gather(values, name, axis=axis, tiled=True)  29.7 us
    psum x1, blocking collectives, local(): packed = lax.psum(packed, 'tensor')  17.2 us
    all_to_all x1, starting transfers between devices, local(): got = lax.all_to_all(send, DP, 0, 0, tiled=True)  12.1 us
    all_to_all x1, starting transfers between devices, local(): squares = jnp.sum(lax.all_to_all(spread, DP, 0, 0, tiled=True))  8.49 us
    all_to_all x1, waiting for transfers between devices, local(): squares = jnp.sum(lax.all_to_all(spread, DP, 0, 0, tiled=True))  7.51 us
    transpose x1, local copies, waits for them, and re-layouts, local(): exp_rows = exp.transpose(1, 0, 2).reshape(e_rows, n_e * e_cols)  5.07 us
  transfers between devices with their start and end apart: 3, of which 3 were waited for; matrix products, arithmetic and copies ran while one was open for 1% of the time, Pallas kernels for 0%

profile of v5, /device:TPU:4, one launch (start us, length us, event | category | flops | bytes accessed | tf_op | source)
XLA Modules:
  0.0 210.2 jit_solution(10380387168854763233)
XLA Ops:
  7.2 0.9 copy.66
  8.1 5.1 %copy.65 = bf16[512,2,1024]{2,1,0:T(2,128)(2,1)} copy(bf16[512,2,1024]{2,0,1:T(8,128)(2,1)} %bitcast.66) | data formatting | bytes 4194304 | tf_op jit(solution)/shard_map/transpose | solution.py:62
  13.2 3.3 %concatenate.16 = bf16[64,8,2048]{2,1,0:T(8,128)(2,1)S(1)} reshape(bf16[512,2,1024]{2,1,0:T(2,128)(2,1)} %copy.65) | data formatting | bytes 4194304 | tf_op jit(solution)/shard_map/concatenate | solution.py:63
  16.5 0.0 copy-done.1
  16.5 1.8 pad_maximum_fusion
  18.3 12.1 %all-to-all-start = ((bf16[64,8,2596]{2,1,0:T(8,128)(2,1)}), bf16[64,8,2596]{2,1,0:T(8,128)(2,1)S(1)}, u32[]{:S(2)}, u32[]{:S(2)}) async-start(bf16[64,8,2596]{2,1,0:T(8,128)(2,1)} %pad_maximum_fusion), calls=%async_computation | async-start | bytes 5505024 | tf_op jit(solution)/shard_map/all_to_all | solution.py:64
  30.4 0.0 copy-start.8
  30.4 0.0 copy-start.9
  30.4 0.0 copy-start.10
  30.4 0.0 copy-start.5
  30.4 0.0 copy-start.6
  30.5 0.0 copy-start.7
  30.5 0.0 copy-start.2
  30.5 0.0 copy-start.3
  30.5 0.0 copy-start.4
  32.5 60.0 %all-to-all-done = bf16[64,8,2596]{2,1,0:T(8,128)(2,1)S(1)} async-done(((bf16[64,8,2596]{2,1,0:T(8,128)(2,1)}), bf16[64,8,2596]{2,1,0:T(8,128)(2,1)S(1)}, u32[]{:S(2)}, u32[]{:S(2)}) %all-to-all-start) | async-done | bytes 2658336 | tf_op jit(solution)/shard_map/all_to_all | solution.py:64
  92.5 0.5 convert_reduce_fusion
  93.1 0.6 multiply_reduce_fusion
  93.7 0.6 multiply_reduce_fusion.1
  95.6 0.1 constant_dynamic-update-slice_fusion.3
  95.7 0.0 copy-done.9
  95.7 0.1 constant_dynamic-update-slice_fusion.2
  95.8 0.0 copy-done.10
  95.8 0.1 constant_dynamic-update-slice_fusion.1
  95.9 17.2 %psum.7 = f32[5,36,8]{1,2,0:T(8,128)S(1)} all-reduce(f32[5,36,8]{1,2,0:T(8,128)S(1)} %constant_dynamic-update-slice_fusion), channel_id=1, replica_groups=mesh['dp_x'=4,'dp_z'=8,'dp_core'=2,'tensor'=4] {'tensor'}, use_global_device_ids=true, to_apply=%region_3.4 | all-reduce | flops 1440 | bytes 11520 | tf_op jit(solution)/shard_map/psum | solution.py:85
  113.1 0.6 multiply_reduce_fusion.2
  113.7 0.5 slice.63
  115.5 0.6 broadcast_in_dim.28
  116.1 8.5 %all-to-all-start.1 = ((f32[64,1,1]{2,1,0:T(1,128)}), f32[64,1,1]{2,1,0:T(1,128)S(1)}, u32[]{:S(2)}, u32[]{:S(2)}) async-start(f32[64,1,1]{2,1,0:T(1,128)} %broadcast_in_dim.28), calls=%async_computation.1 | async-start | bytes 65536 | tf_op jit(solution)/shard_map/all_to_all | solution.py:91
  124.6 0.0 all-gather.2.cloned.1.call-start
  124.8 7.5 %all-to-all-done.1 = f32[64,1,1]{2,1,0:T(1,128)S(1)} async-done(((f32[64,1,1]{2,1,0:T(1,128)}), f32[64,1,1]{2,1,0:T(1,128)S(1)}, u32[]{:S(2)}, u32[]{:S(2)}) %all-to-all-start.1) | async-done | bytes 288 | tf_op jit(solution)/shard_map/all_to_all | solution.py:91
  132.3 0.7 reduce_sum.49
  133.7 0.0 copy-done.5
  133.7 0.0 copy-done.6
  133.7 0.0 copy-done.7
  133.8 0.6 fusion.7
  134.4 0.7 fusion.9
  135.1 1.9 all_gather.9
  137.0 27.9 %all_gather.10 = bf16[128,2596]{1,0:T(8,128)(2,1)} all-gather(bf16[16,2596]{1,0:T(8,128)(2,1)S(1)} %all_gather.9), channel_id=1, replica_groups=mesh['dp_x'=4,'dp_z'=8,'dp_core'=2,'tensor'=4] {'dp_z'}, dimensions={0}, use_global_device_ids=true | all-gather | bytes 747648 | tf_op jit(solution)/shard_map/all_gather | solution.py:120
  164.8 0.0 all-gather.2.cloned.1.call-update
  164.9 0.6 constant_dynamic-slice_fusion.2
  165.4 0.6 constant_dynamic-slice_fusion
  166.0 32.2 %all-gather.2.cloned.1.call-done = bf16[512,2596]{1,0:T(8,128)(2,1)} async-done(((bf16[128,2596]{1,0:T(8,128)(2,1)}), bf16[512,2596]{1,0:T(8,128)(2,1)}) %all-gather.2.cloned.1.call-update) | async-done | bytes 2658320 | tf_op jit(solution)/shard_map/all_gather | solution.py:120
  198.2 1.1 slice_bitcast_fusion
  199.3 0.7 copy.69
  200.0 1.5 copy.73
  201.5 1.0 copy-done
  202.5 0.8 slice.68
  (18 shorter events, 0.1 us)
Async XLA Ops:
  13.2 3.4 %copy-start.1 = (bf16[1,1,512,512]{3,2,1,0:T(8,128)(2,1)S(1)}, bf16[1,1,512,512]{3,2,1,0:T(8,128)(2,1)}, u32[]{:S(2)}) copy-start(bf16[1,1,512,512]{3,2,1,0:T(8,128)(2,1)} %param.17) | copy-start | bytes 1572868
  18.3 74.2 %all-to-all-start = ((bf16[64,8,2596]{2,1,0:T(8,128)(2,1)}), bf16[64,8,2596]{2,1,0:T(8,128)(2,1)S(1)}, u32[]{:S(2)}, u32[]{:S(2)}) async-start(bf16[64,8,2596]{2,1,0:T(8,128)(2,1)} %pad_maximum_fusion), calls=%async_computation | async-start | bytes 5505024 | tf_op jit(solution)/shard_map/all_to_all | solution.py:64
  30.4 65.2 %copy-start.8 = (f32[36,2]{0,1:T(2,128)S(1)}, f32[36,2]{0,1:T(2,128)}, u32[]{:S(2)}) copy-start(f32[36,2]{0,1:T(2,128)} %param.26) | copy-start | bytes 868
  30.4 65.3 %copy-start.9 = (f32[36,2]{0,1:T(2,128)S(1)}, f32[36,2]{0,1:T(2,128)}, u32[]{:S(2)}) copy-start(f32[36,2]{0,1:T(2,128)} %param.27) | copy-start | bytes 868
  30.4 65.4 %copy-start.10 = (f32[36,2]{0,1:T(2,128)S(1)}, f32[36,2]{0,1:T(2,128)}, u32[]{:S(2)}) copy-start(f32[36,2]{0,1:T(2,128)} %param.28) | copy-start | bytes 868
  30.4 103.3 %copy-start.5 = (f32[8,512]{1,0:T(8,128)S(1)}, f32[8,512]{1,0:T(8,128)}, u32[]{:S(2)}) copy-start(f32[8,512]{1,0:T(8,128)} %param.20) | copy-start | bytes 49156
  30.4 103.3 %copy-start.6 = (f32[8,512]{1,0:T(8,128)S(1)}, f32[8,512]{1,0:T(8,128)}, u32[]{:S(2)}) copy-start(f32[8,512]{1,0:T(8,128)} %param.22) | copy-start | bytes 49156
  30.5 103.3 %copy-start.7 = (f32[8,512]{1,0:T(8,128)S(1)}, f32[8,512]{1,0:T(8,128)}, u32[]{:S(2)}) copy-start(f32[8,512]{1,0:T(8,128)} %param.21) | copy-start | bytes 49156
  30.5 103.9 %copy-start.2 = (f32[2,8,1024]{2,1,0:T(8,128)S(1)}, f32[2,8,1024]{2,1,0:T(8,128)}, u32[]{:S(2)}) copy-start(f32[2,8,1024]{2,1,0:T(8,128)} %param.23) | copy-start | bytes 196612
  30.5 103.9 %copy-start.3 = (f32[2,8,1024]{2,1,0:T(8,128)S(1)}, f32[2,8,1024]{2,1,0:T(8,128)}, u32[]{:S(2)}) copy-start(f32[2,8,1024]{2,1,0:T(8,128)} %param.25) | copy-start | bytes 196612
  30.5 103.9 %copy-start.4 = (f32[2,8,1024]{2,1,0:T(8,128)S(1)}, f32[2,8,1024]{2,1,0:T(8,128)}, u32[]{:S(2)}) copy-start(f32[2,8,1024]{2,1,0:T(8,128)} %param.24) | copy-start | bytes 196612
  116.1 16.1 %all-to-all-start.1 = ((f32[64,1,1]{2,1,0:T(1,128)}), f32[64,1,1]{2,1,0:T(1,128)S(1)}, u32[]{:S(2)}, u32[]{:S(2)}) async-start(f32[64,1,1]{2,1,0:T(1,128)} %broadcast_in_dim.28), calls=%async_computation.1 | async-start | bytes 65536 | tf_op jit(solution)/shard_map/all_to_all | solution.py:91
  124.6 73.6 %all-gather.2.cloned.1.call-start = ((), (), s32[]{:S(2)}) async-start(), calls=%async_computation.2 | async-start | bytes 3440640 | tf_op jit(solution)/shard_map/all_gather | solution.py:120
  198.2 1.8 slice-start
  200.0 2.5 %copy-start = (bf16[512,2596]{1,0:T(8,128)(2,1)S(1)}, bf16[512,2596]{1,0:T(8,128)(2,1)}, u32[]{:S(2)}) copy-start(bf16[512,2596]{1,0:T(8,128)(2,1)} %all-gather.2.cloned.1.call-done) | copy-start | bytes 7974916
Sparse Core Ops, SparseCore 0:
  165.0 33.1 all-gather.1

commit v6 on v5

--- a/solution.py
+++ b/solution.py
@@ -59,13 +59,13 @@
     rc = r_cols // n_dp
     own = rc // n_t
 
-    exp_rows = exp.transpose(1, 0, 2).reshape(e_rows, n_e * e_cols)
-    send = jnp.concatenate([att, exp_rows, rte.T], axis=1)
+    send = jnp.concatenate([att, rte.T], axis=1)
     got = lax.all_to_all(send, DP, 0, 0, tiled=True)
+    exp_got = lax.all_to_all(exp, DP, 1, 1, tiled=True)
     total = jnp.sum(got.reshape(n_dp, ra, -1).astype(jnp.float32), axis=0)
     attention_sum = total[:, :cols]
-    expert_sum = total[:, cols : cols + n_e * e_cols].reshape(re, n_e, e_cols).transpose(1, 0, 2)
-    route_part = total[:, cols + n_e * e_cols :].T
+    route_part = total[:, cols:].T
+    expert_sum = jnp.sum(exp_got.reshape(n_e, n_dp, re, e_cols).astype(jnp.float32), axis=1)
 
     local_squares = jnp.sum(attention_sum * attention_sum) + jnp.sum(expert_sum * expert_sum)
     slot = (jnp.arange(rc) // own == t_idx)[None, :]

time: 213 us -> 219 us (1.028)
  starting transfers between devices: 20.6 us -> 27.8 us
  local copies, waits for them, and re-layouts: 16.9 us -> 13.5 us
    all_to_all x0 -> x1, waiting for transfers between devices: none -> 45.5 us  [local(): exp_got = lax.all_to_all(exp, DP, 1, 1, tiled=True)]
    all_to_all x1, waiting for transfers between devices: 60 us -> 15.8 us  [local(): got = lax.all_to_all(send, DP, 0, 0, tiled=True)]
    all_to_all x0 -> x1, starting transfers between devices: none -> 7.19 us  [local(): exp_got = lax.all_to_all(exp, DP, 1, 1, tiled=True)]
    transpose x2 -> x1, local copies, waits for them, and re-layouts: 5.99 us -> 1.07 us  [local(): send = jnp.concatenate([att, rte.T], axis=1)]
    unnamed x24 -> x25, local copies, waits for them, and re-layouts: 1.81 us -> 5.31 us
    concatenate x1 -> x0, local copies, waits for them, and re-layouts: 3.35 us -> none  [local(): send = jnp.concatenate([att, exp_rows, rte.T], axis=1)]
  transfers between devices with their start and end apart: 3 -> 4, of which waited for: 3 -> 4; matrix products, arithmetic and copies ran while one was open for 1% -> 3% of each run, Pallas kernels for 0% -> 0%
where the time goes in v6:
time: 219 us; the launch traced here: 217 us
  waiting for transfers between devices  101 us (46%)
  blocking collectives  47 us (21%)
  starting transfers between devices  27.8 us (13%)
  between operations  19.6 us (9%)
  local copies, waits for them, and re-layouts  13.5 us (6%)
  other arithmetic  7.91 us (4%)
    all_to_all x1, waiting for transfers between devices, local(): exp_got = lax.all_to_all(exp, DP, 1, 1, tiled=True)  45.5 us
    all_gather x1, waiting for transfers between devices, gather(): values = lax.all_gather(values, name, axis=axis, tiled=True)  32.2 us
    all_gather x2, blocking collectives, gather(): values = lax.all_gather(values, name, axis=axis, tiled=True)  29.7 us
    psum x1, blocking collectives, local(): packed = lax.psum(packed, 'tensor')  17.2 us
    all_to_all x1, waiting for transfers between devices, local(): got = lax.all_to_all(send, DP, 0, 0, tiled=True)  15.8 us
    all_to_all x1, starting transfers between devices, local(): got = lax.all_to_all(send, DP, 0, 0, tiled=True)  12.1 us
    all_to_all x1, starting transfers between devices, local(): squares = jnp.sum(lax.all_to_all(spread, DP, 0, 0, tiled=True))  8.44 us
    all_to_all x1, waiting for transfers between devices, local(): squares = jnp.sum(lax.all_to_all(spread, DP, 0, 0, tiled=True))  7.51 us
  transfers between devices with their start and end apart: 4, of which 4 were waited for; matrix products, arithmetic and copies ran while one was open for 3% of the time, Pallas kernels for 0%

profile of v6, /device:TPU:4, one launch (start us, length us, event | category | flops | bytes accessed | tf_op | source)
XLA Modules:
  0.0 216.8 jit_solution(18354777785506324831)
XLA Ops:
  7.2 0.0 copy-start.1
  7.2 1.1 copy.93
  8.3 1.9 pad_maximum_fusion
  10.2 12.1 %all-to-all-start = ((bf16[64,8,548]{2,1,0:T(8,128)(2,1)}), bf16[64,8,548]{2,1,0:T(8,128)(2,1)S(1)}, u32[]{:S(2)}, u32[]{:S(2)}) async-start(bf16[64,8,548]{2,1,0:T(8,128)(2,1)} %pad_maximum_fusion), calls=%async_computation | async-start | bytes 1310720 | tf_op jit(solution)/shard_map/all_to_all | solution.py:63
  22.3 0.0 copy-done.1
  22.3 3.5 %copy.111 = bf16[1,1,2,512,1024]{4,2,3,1,0:T(2,128)(2,1)} copy(bf16[1,1,2,512,1024]{4,3,2,1,0:T(8,128)(2,1)S(1)} %copy-done.1) | data formatting | bytes 4194304 | tf_op args[1]
  25.8 15.8 %all-to-all-done = bf16[64,8,548]{2,1,0:T(8,128)(2,1)S(1)} async-done(((bf16[64,8,548]{2,1,0:T(8,128)(2,1)}), bf16[64,8,548]{2,1,0:T(8,128)(2,1)S(1)}, u32[]{:S(2)}, u32[]{:S(2)}) %all-to-all-start) | async-done | bytes 561184 | tf_op jit(solution)/shard_map/all_to_all | solution.py:63
  41.6 7.2 %all-to-all-start.1 = ((bf16[2,512,1024]{2,0,1:T(2,128)(2,1)}), bf16[2,512,1024]{2,0,1:T(2,128)(2,1)S(1)}, u32[]{:S(2)}, u32[]{:S(2)}) async-start(bf16[2,512,1024]{2,0,1:T(2,128)(2,1)} %bitcast.60), calls=%async_computation.1 | async-start | bytes 4194304 | tf_op jit(solution)/shard_map/all_to_all | solution.py:64
  48.8 0.0 copy-start.5
  48.8 0.0 copy-start.6
  48.8 0.0 copy-start.7
  48.8 0.0 copy-start.2
  48.9 0.0 copy-start.3
  48.9 0.0 copy-start.4
  50.9 0.1 convert_reduce_fusion.1
  51.0 0.6 multiply_reduce_fusion.1
  51.6 0.0 copy-done.8
  51.6 0.1 constant_dynamic-update-slice_fusion.3
  51.7 0.0 copy-done.9
  51.7 0.1 constant_dynamic-update-slice_fusion.2
  51.8 0.0 copy-done.10
  51.8 0.1 constant_dynamic-update-slice_fusion.1
  51.9 45.5 %all-to-all-done.1 = bf16[2,512,1024]{2,0,1:T(2,128)(2,1)S(1)} async-done(((bf16[2,512,1024]{2,0,1:T(2,128)(2,1)}), bf16[2,512,1024]{2,0,1:T(2,128)(2,1)S(1)}, u32[]{:S(2)}, u32[]{:S(2)}) %all-to-all-start.1) | async-done | bytes 2097184 | tf_op jit(solution)/shard_map/all_to_all | solution.py:64
  97.4 1.7 convert_reduce_fusion
  99.1 0.7 multiply_reduce_fusion
  101.0 17.2 %psum.7 = f32[5,36,8]{1,2,0:T(8,128)S(1)} all-reduce(f32[5,36,8]{1,2,0:T(8,128)S(1)} %constant_dynamic-update-slice_fusion), channel_id=1, replica_groups=mesh['dp_x'=4,'dp_z'=8,'dp_core'=2,'tensor'=4] {'tensor'}, use_global_device_ids=true, to_apply=%region_4.5 | all-reduce | flops 1440 | bytes 11520 | tf_op jit(solution)/shard_map/psum | solution.py:85
  118.3 0.6 multiply_reduce_fusion.2
  118.9 0.5 slice.58
  120.7 0.6 broadcast_in_dim.28
  121.3 8.4 %all-to-all-start.2 = ((f32[64,1,1]{2,1,0:T(1,128)}), f32[64,1,1]{2,1,0:T(1,128)S(1)}, u32[]{:S(2)}, u32[]{:S(2)}) async-start(f32[64,1,1]{2,1,0:T(1,128)} %broadcast_in_dim.28), calls=%async_computation.2 | async-start | bytes 65536 | tf_op jit(solution)/shard_map/all_to_all | solution.py:91
  129.8 0.0 all-gather.2.cloned.1.call-start
  129.9 7.5 %all-to-all-done.2 = f32[64,1,1]{2,1,0:T(1,128)S(1)} async-done(((f32[64,1,1]{2,1,0:T(1,128)}), f32[64,1,1]{2,1,0:T(1,128)S(1)}, u32[]{:S(2)}, u32[]{:S(2)}) %all-to-all-start.2) | async-done | bytes 288 | tf_op jit(solution)/shard_map/all_to_all | solution.py:91
  137.4 0.7 reduce_sum.59
  138.9 0.0 copy-done.5
  138.9 0.6 fusion.7
  139.5 0.7 fusion.9
  140.3 1.9 all_gather.9
  142.1 27.9 %all_gather.10 = bf16[128,2596]{1,0:T(8,128)(2,1)} all-gather(bf16[16,2596]{1,0:T(8,128)(2,1)S(1)} %all_gather.9), channel_id=1, replica_groups=mesh['dp_x'=4,'dp_z'=8,'dp_core'=2,'tensor'=4] {'dp_z'}, dimensions={0}, use_global_device_ids=true | all-gather | bytes 747648 | tf_op jit(solution)/shard_map/all_gather | solution.py:120
  170.0 0.0 all-gather.2.cloned.1.call-update
  170.0 0.6 constant_dynamic-slice_fusion.2
  170.6 0.6 constant_dynamic-slice_fusion
  171.2 32.2 %all-gather.2.cloned.1.call-done = bf16[512,2596]{1,0:T(8,128)(2,1)} async-done(((bf16[128,2596]{1,0:T(8,128)(2,1)}), bf16[512,2596]{1,0:T(8,128)(2,1)}) %all-gather.2.cloned.1.call-update) | async-done | bytes 2658320 | tf_op jit(solution)/shard_map/all_gather | solution.py:120
  203.4 0.9 slice_bitcast_fusion
  204.3 0.7 copy.98
  205.0 1.6 slice-done
  206.6 1.5 copy.110
  208.1 1.0 copy-done
  209.1 0.8 slice.63
  (19 shorter events, 0.1 us)
Async XLA Ops:
  7.2 15.1 %copy-start.1 = (bf16[1,1,2,512,1024]{4,3,2,1,0:T(8,128)(2,1)S(1)}, bf16[1,1,2,512,1024]{4,3,2,1,0:T(8,128)(2,1)}, u32[]{:S(2)}) copy-start(bf16[1,1,2,512,1024]{4,3,2,1,0:T(8,128)(2,1)} %param.18) | copy-start | bytes 6291460
  10.2 31.4 %all-to-all-start = ((bf16[64,8,548]{2,1,0:T(8,128)(2,1)}), bf16[64,8,548]{2,1,0:T(8,128)(2,1)S(1)}, u32[]{:S(2)}, u32[]{:S(2)}) async-start(bf16[64,8,548]{2,1,0:T(8,128)(2,1)} %pad_maximum_fusion), calls=%async_computation | async-start | bytes 1310720 | tf_op jit(solution)/shard_map/all_to_all | solution.py:63
  41.6 10.0 %copy-start.8 = (f32[36,2]{0,1:T(2,128)S(1)}, f32[36,2]{0,1:T(2,128)}, u32[]{:S(2)}) copy-start(f32[36,2]{0,1:T(2,128)} %param.26) | copy-start | bytes 868
  41.6 10.1 %copy-start.9 = (f32[36,2]{0,1:T(2,128)S(1)}, f32[36,2]{0,1:T(2,128)}, u32[]{:S(2)}) copy-start(f32[36,2]{0,1:T(2,128)} %param.27) | copy-start | bytes 868
  41.6 10.2 %copy-start.10 = (f32[36,2]{0,1:T(2,128)S(1)}, f32[36,2]{0,1:T(2,128)}, u32[]{:S(2)}) copy-start(f32[36,2]{0,1:T(2,128)} %param.28) | copy-start | bytes 868
  41.6 55.8 %all-to-all-start.1 = ((bf16[2,512,1024]{2,0,1:T(2,128)(2,1)}), bf16[2,512,1024]{2,0,1:T(2,128)(2,1)S(1)}, u32[]{:S(2)}, u32[]{:S(2)}) async-start(bf16[2,512,1024]{2,0,1:T(2,128)(2,1)} %bitcast.60), calls=%async_computation.1 | async-start | bytes 4194304 | tf_op jit(solution)/shard_map/all_to_all | solution.py:64
  48.8 90.1 %copy-start.5 = (f32[8,512]{1,0:T(8,128)S(1)}, f32[8,512]{1,0:T(8,128)}, u32[]{:S(2)}) copy-start(f32[8,512]{1,0:T(8,128)} %param.20) | copy-start | bytes 49156
  48.8 90.1 %copy-start.6 = (f32[8,512]{1,0:T(8,128)S(1)}, f32[8,512]{1,0:T(8,128)}, u32[]{:S(2)}) copy-start(f32[8,512]{1,0:T(8,128)} %param.22) | copy-start | bytes 49156
  48.8 90.1 %copy-start.7 = (f32[8,512]{1,0:T(8,128)S(1)}, f32[8,512]{1,0:T(8,128)}, u32[]{:S(2)}) copy-start(f32[8,512]{1,0:T(8,128)} %param.21) | copy-start | bytes 49156
  48.8 90.7 %copy-start.2 = (f32[2,8,1024]{2,1,0:T(8,128)S(1)}, f32[2,8,1024]{2,1,0:T(8,128)}, u32[]{:S(2)}) copy-start(f32[2,8,1024]{2,1,0:T(8,128)} %param.23) | copy-start | bytes 196612
  48.9 90.7 %copy-start.3 = (f32[2,8,1024]{2,1,0:T(8,128)S(1)}, f32[2,8,1024]{2,1,0:T(8,128)}, u32[]{:S(2)}) copy-start(f32[2,8,1024]{2,1,0:T(8,128)} %param.25) | copy-start | bytes 196612
  48.9 90.7 %copy-start.4 = (f32[2,8,1024]{2,1,0:T(8,128)S(1)}, f32[2,8,1024]{2,1,0:T(8,128)}, u32[]{:S(2)}) copy-start(f32[2,8,1024]{2,1,0:T(8,128)} %param.24) | copy-start | bytes 196612
  121.3 16.1 %all-to-all-start.2 = ((f32[64,1,1]{2,1,0:T(1,128)}), f32[64,1,1]{2,1,0:T(1,128)S(1)}, u32[]{:S(2)}, u32[]{:S(2)}) async-start(f32[64,1,1]{2,1,0:T(1,128)} %broadcast_in_dim.28), calls=%async_computation.2 | async-start | bytes 65536 | tf_op jit(solution)/shard_map/all_to_all | solution.py:91
  129.8 73.6 %all-gather.2.cloned.1.call-start = ((), (), s32[]{:S(2)}) async-start(), calls=%async_computation.3 | async-start | bytes 3440640 | tf_op jit(solution)/shard_map/all_gather | solution.py:120
  205.0 1.6 slice-start
  206.6 2.5 %copy-start = (bf16[512,2596]{1,0:T(8,128)(2,1)S(1)}, bf16[512,2596]{1,0:T(8,128)(2,1)}, u32[]{:S(2)}) copy-start(bf16[512,2596]{1,0:T(8,128)(2,1)} %all-gather.2.cloned.1.call-done) | copy-start | bytes 7974916
Sparse Core Ops, SparseCore 0:
  170.1 33.1 all-gather.1

commit v7 on v5

--- a/solution.py
+++ b/solution.py
@@ -115,10 +115,12 @@
     def mine(values):
         return lax.dynamic_slice_in_dim(values, t_idx * own, own, axis=1)
 
-    def gather(values, axis):
-        for name in reversed(DP_PARTS):
-            values = lax.all_gather(values, name, axis=axis, tiled=True)
-        return values
+    def gather(values):
+        sizes = [lax.axis_size(name) for name in DP_PARTS]
+        for name in (DP_PARTS[1], DP_PARTS[0], DP_PARTS[2]):
+            values = lax.all_gather(values, name, axis=0, tiled=True)
+        blocks = values.reshape(sizes[2], sizes[0], sizes[1], -1, values.shape[-1])
+        return blocks.transpose(1, 2, 0, 3, 4).reshape(values.shape)
 
     rest = jnp.concatenate(
         [
@@ -128,7 +130,7 @@
         ],
         axis=1,
     )
-    rest = gather(rest, 0)
+    rest = gather(rest)
     attention_served = rest[:, :cols]
     expert_served = (
         rest[:, cols : cols + n_e * e_cols].reshape(e_rows, n_e, e_cols).transpose(1, 0, 2)

time: 213 us -> 219 us (1.028)
  waiting for transfers between devices: 99.7 us -> 109 us
  blocking collectives: 47 us -> 44.2 us
    all_gather x1 -> x2, waiting for transfers between devices: 32.2 us -> 41.4 us  [gather(): values = lax.all_gather(values, name, axis=0, tiled=True)]
    all_gather x2 -> x1, blocking collectives: 29.7 us -> 26.9 us  [gather(): values = lax.all_gather(values, name, axis=0, tiled=True)]
  transfers between devices with their start and end apart: 3 -> 4, of which waited for: 3 -> 4; matrix products, arithmetic and copies ran while one was open for 1% -> 1% of each run, Pallas kernels for 0% -> 0%
where the time goes in v7:
time: 219 us; the launch traced here: 217 us
  waiting for transfers between devices  109 us (50%)
  blocking collectives  44.2 us (20%)
  starting transfers between devices  20.7 us (9%)
  between operations  19.7 us (9%)
  local copies, waits for them, and re-layouts  17 us (8%)
  other arithmetic  6.39 us (3%)
    all_to_all x1, waiting for transfers between devices, local(): got = lax.all_to_all(send, DP, 0, 0, tiled=True)  60 us
    all_gather x2, waiting for transfers between devices, gather(): values = lax.all_gather(values, name, axis=0, tiled=True)  41.4 us
    all_gather x1, blocking collectives, gather(): values = lax.all_gather(values, name, axis=0, tiled=True)  26.9 us
    psum x1, blocking collectives, local(): packed = lax.psum(packed, 'tensor')  17.2 us
    all_to_all x1, starting transfers between devices, local(): got = lax.all_to_all(send, DP, 0, 0, tiled=True)  12.1 us
    all_to_all x1, starting transfers between devices, local(): squares = jnp.sum(lax.all_to_all(spread, DP, 0, 0, tiled=True))  8.49 us
    all_to_all x1, waiting for transfers between devices, local(): squares = jnp.sum(lax.all_to_all(spread, DP, 0, 0, tiled=True))  7.51 us
    transpose x1, local copies, waits for them, and re-layouts, local(): exp_rows = exp.transpose(1, 0, 2).reshape(e_rows, n_e * e_cols)  5.07 us
  transfers between devices with their start and end apart: 4, of which 4 were waited for; matrix products, arithmetic and copies ran while one was open for 1% of the time, Pallas kernels for 0%

profile of v7, /device:TPU:4, one launch (start us, length us, event | category | flops | bytes accessed | tf_op | source)
XLA Modules:
  0.0 216.9 jit_solution(14182298504728596153)
XLA Ops:
  7.2 0.9 copy.41
  8.1 5.1 %copy.40 = bf16[512,2,1024]{2,1,0:T(2,128)(2,1)} copy(bf16[512,2,1024]{2,0,1:T(8,128)(2,1)} %bitcast.74) | data formatting | bytes 4194304 | tf_op jit(solution)/shard_map/transpose | solution.py:62
  13.2 3.3 %concatenate.16 = bf16[64,8,2048]{2,1,0:T(8,128)(2,1)S(1)} reshape(bf16[512,2,1024]{2,1,0:T(2,128)(2,1)} %copy.40) | data formatting | bytes 4194304 | tf_op jit(solution)/shard_map/concatenate | solution.py:63
  16.5 1.8 pad_maximum_fusion
  18.3 12.1 %all-to-all-start = ((bf16[64,8,2596]{2,1,0:T(8,128)(2,1)}), bf16[64,8,2596]{2,1,0:T(8,128)(2,1)S(1)}, u32[]{:S(2)}, u32[]{:S(2)}) async-start(bf16[64,8,2596]{2,1,0:T(8,128)(2,1)} %pad_maximum_fusion), calls=%async_computation | async-start | bytes 5505024 | tf_op jit(solution)/shard_map/all_to_all | solution.py:64
  30.4 0.0 copy-start.7
  30.4 0.0 copy-start.8
  30.4 0.0 copy-start.9
  30.4 0.0 copy-start.4
  30.4 0.0 copy-start.5
  30.5 0.0 copy-start.6
  30.5 0.0 copy-start.1
  30.5 0.0 copy-start.2
  30.5 0.0 copy-start.3
  32.5 60.0 %all-to-all-done = bf16[64,8,2596]{2,1,0:T(8,128)(2,1)S(1)} async-done(((bf16[64,8,2596]{2,1,0:T(8,128)(2,1)}), bf16[64,8,2596]{2,1,0:T(8,128)(2,1)S(1)}, u32[]{:S(2)}, u32[]{:S(2)}) %all-to-all-start) | async-done | bytes 2658336 | tf_op jit(solution)/shard_map/all_to_all | solution.py:64
  92.5 0.5 convert_reduce_fusion
  93.1 0.6 multiply_reduce_fusion
  93.7 0.6 multiply_reduce_fusion.1
  95.6 0.1 constant_dynamic-update-slice_fusion.3
  95.7 0.0 copy-done.8
  95.7 0.1 constant_dynamic-update-slice_fusion.2
  95.8 0.0 copy-done.9
  95.8 0.1 constant_dynamic-update-slice_fusion.1
  95.9 17.2 %psum.7 = f32[5,36,8]{1,2,0:T(8,128)S(1)} all-reduce(f32[5,36,8]{1,2,0:T(8,128)S(1)} %constant_dynamic-update-slice_fusion), channel_id=1, replica_groups=mesh['dp_x'=4,'dp_z'=8,'dp_core'=2,'tensor'=4] {'tensor'}, use_global_device_ids=true, to_apply=%region_3.4 | all-reduce | flops 1440 | bytes 11520 | tf_op jit(solution)/shard_map/psum | solution.py:85
  113.1 0.6 multiply_reduce_fusion.2
  113.7 0.5 slice.63
  115.5 0.6 broadcast_in_dim.28
  116.1 8.5 %all-to-all-start.1 = ((f32[64,1,1]{2,1,0:T(1,128)}), f32[64,1,1]{2,1,0:T(1,128)S(1)}, u32[]{:S(2)}, u32[]{:S(2)}) async-start(f32[64,1,1]{2,1,0:T(1,128)} %broadcast_in_dim.28), calls=%async_computation.1 | async-start | bytes 65536 | tf_op jit(solution)/shard_map/all_to_all | solution.py:91
  124.6 0.0 all-gather.3.cloned.1.call-start
  124.8 7.5 %all-to-all-done.1 = f32[64,1,1]{2,1,0:T(1,128)S(1)} async-done(((f32[64,1,1]{2,1,0:T(1,128)}), f32[64,1,1]{2,1,0:T(1,128)S(1)}, u32[]{:S(2)}, u32[]{:S(2)}) %all-to-all-start.1) | async-done | bytes 288 | tf_op jit(solution)/shard_map/all_to_all | solution.py:91
  132.3 0.7 reduce_sum.49
  133.7 0.0 copy-done.4
  133.7 0.0 copy-done.5
  133.8 0.6 fusion.7
  134.4 0.7 fusion.9
  135.1 26.9 %all_gather.9 = bf16[64,2596]{1,0:T(8,128)(2,1)} all-gather(bf16[8,2596]{1,0:T(8,128)(2,1)S(1)} %pad_maximum_fusion.1), channel_id=1, replica_groups=mesh['dp_x'=4,'dp_z'=8,'dp_core'=2,'tensor'=4] {'dp_z'}, dimensions={0}, use_global_device_ids=true | all-gather | bytes 373824 | tf_op jit(solution)/shard_map/all_gather | solution.py:121
  162.0 0.0 all-gather.3.cloned.1.call-update
  162.1 0.0 all-gather.5.cloned.1.call-start
  162.1 22.6 %all-gather.3.cloned.1.call-done = bf16[256,2596]{1,0:T(8,128)(2,1)} async-done(((bf16[64,2596]{1,0:T(8,128)(2,1)}), bf16[256,2596]{1,0:T(8,128)(2,1)}) %all-gather.3.cloned.1.call-update) | async-done | bytes 1329168 | tf_op jit(solution)/shard_map/all_gather | solution.py:121
  184.7 0.0 all-gather.5.cloned.1.call-update
  184.7 0.6 constant_dynamic-slice_fusion.2
  185.3 0.6 constant_dynamic-slice_fusion
  185.9 18.8 %all-gather.5.cloned.1.call-done = bf16[512,2596]{1,0:T(8,128)(2,1)} async-done(((bf16[256,2596]{1,0:T(8,128)(2,1)}), bf16[512,2596]{1,0:T(8,128)(2,1)}) %all-gather.5.cloned.1.call-update) | async-done | bytes 2658320 | tf_op jit(solution)/shard_map/all_gather | solution.py:121
  204.7 2.0 copy.43
  206.7 0.8 slice.68
  207.5 0.3 slice.69
  207.8 0.7 copy.45
  208.6 1.5 copy.49
  (18 shorter events, 0.1 us)
Async XLA Ops:
  13.2 3.4 %copy-start = (bf16[1,1,512,512]{3,2,1,0:T(8,128)(2,1)S(1)}, bf16[1,1,512,512]{3,2,1,0:T(8,128)(2,1)}, u32[]{:S(2)}) copy-start(bf16[1,1,512,512]{3,2,1,0:T(8,128)(2,1)} %param.17) | copy-start | bytes 1572868
  18.3 74.2 %all-to-all-start = ((bf16[64,8,2596]{2,1,0:T(8,128)(2,1)}), bf16[64,8,2596]{2,1,0:T(8,128)(2,1)S(1)}, u32[]{:S(2)}, u32[]{:S(2)}) async-start(bf16[64,8,2596]{2,1,0:T(8,128)(2,1)} %pad_maximum_fusion), calls=%async_computation | async-start | bytes 5505024 | tf_op jit(solution)/shard_map/all_to_all | solution.py:64
  30.4 65.2 %copy-start.7 = (f32[36,2]{0,1:T(2,128)S(1)}, f32[36,2]{0,1:T(2,128)}, u32[]{:S(2)}) copy-start(f32[36,2]{0,1:T(2,128)} %param.26) | copy-start | bytes 868
  30.4 65.3 %copy-start.8 = (f32[36,2]{0,1:T(2,128)S(1)}, f32[36,2]{0,1:T(2,128)}, u32[]{:S(2)}) copy-start(f32[36,2]{0,1:T(2,128)} %param.27) | copy-start | bytes 868
  30.4 65.4 %copy-start.9 = (f32[36,2]{0,1:T(2,128)S(1)}, f32[36,2]{0,1:T(2,128)}, u32[]{:S(2)}) copy-start(f32[36,2]{0,1:T(2,128)} %param.28) | copy-start | bytes 868
  30.4 103.3 %copy-start.4 = (f32[8,512]{1,0:T(8,128)S(1)}, f32[8,512]{1,0:T(8,128)}, u32[]{:S(2)}) copy-start(f32[8,512]{1,0:T(8,128)} %param.20) | copy-start | bytes 49156
  30.4 103.3 %copy-start.5 = (f32[8,512]{1,0:T(8,128)S(1)}, f32[8,512]{1,0:T(8,128)}, u32[]{:S(2)}) copy-start(f32[8,512]{1,0:T(8,128)} %param.22) | copy-start | bytes 49156
  30.5 103.3 %copy-start.6 = (f32[8,512]{1,0:T(8,128)S(1)}, f32[8,512]{1,0:T(8,128)}, u32[]{:S(2)}) copy-start(f32[8,512]{1,0:T(8,128)} %param.21) | copy-start | bytes 49156
  30.5 103.9 %copy-start.1 = (f32[2,8,1024]{2,1,0:T(8,128)S(1)}, f32[2,8,1024]{2,1,0:T(8,128)}, u32[]{:S(2)}) copy-start(f32[2,8,1024]{2,1,0:T(8,128)} %param.23) | copy-start | bytes 196612
  30.5 103.9 %copy-start.2 = (f32[2,8,1024]{2,1,0:T(8,128)S(1)}, f32[2,8,1024]{2,1,0:T(8,128)}, u32[]{:S(2)}) copy-start(f32[2,8,1024]{2,1,0:T(8,128)} %param.25) | copy-start | bytes 196612
  30.5 103.9 %copy-start.3 = (f32[2,8,1024]{2,1,0:T(8,128)S(1)}, f32[2,8,1024]{2,1,0:T(8,128)}, u32[]{:S(2)}) copy-start(f32[2,8,1024]{2,1,0:T(8,128)} %param.24) | copy-start | bytes 196612
  116.1 16.1 %all-to-all-start.1 = ((f32[64,1,1]{2,1,0:T(1,128)}), f32[64,1,1]{2,1,0:T(1,128)S(1)}, u32[]{:S(2)}, u32[]{:S(2)}) async-start(f32[64,1,1]{2,1,0:T(1,128)} %broadcast_in_dim.28), calls=%async_computation.1 | async-start | bytes 65536 | tf_op jit(solution)/shard_map/all_to_all | solution.py:91
  124.6 60.1 %all-gather.3.cloned.1.call-start = ((), (), s32[]{:S(2)}) async-start(), calls=%async_computation.2 | async-start | bytes 1720320 | tf_op jit(solution)/shard_map/all_gather | solution.py:121
  162.1 42.6 %all-gather.5.cloned.1.call-start = ((), (), s32[]{:S(2)}) async-start(), calls=%async_computation.3 | async-start | bytes 4128768 | tf_op jit(solution)/shard_map/all_gather | solution.py:121
Sparse Core Ops, SparseCore 0:
  162.2 22.4 all-gather.2
  186.5 18.1 all-gather.4

commit v8 on v7

--- a/solution.py
+++ b/solution.py
@@ -116,11 +116,17 @@
         return lax.dynamic_slice_in_dim(values, t_idx * own, own, axis=1)
 
     def gather(values):
-        sizes = [lax.axis_size(name) for name in DP_PARTS]
-        for name in (DP_PARTS[1], DP_PARTS[0], DP_PARTS[2]):
+        for name in (DP_PARTS[2], DP_PARTS[1]):
             values = lax.all_gather(values, name, axis=0, tiled=True)
-        blocks = values.reshape(sizes[2], sizes[0], sizes[1], -1, values.shape[-1])
-        return blocks.transpose(1, 2, 0, 3, 4).reshape(values.shape)
+        name = DP_PARTS[0]
+        size = lax.axis_size(name)
+        ring = [values] + [
+            lax.ppermute(values, name, [(i, (i + size - k) % size) for i in range(size)])
+            for k in range(1, size)
+        ]
+        stacked = jnp.stack(ring)
+        stacked = jnp.roll(stacked, lax.axis_index(name), axis=0)
+        return stacked.reshape((-1,) + values.shape[1:])
 
     rest = jnp.concatenate(
         [

time: 219 us -> 200 us (0.913)
  waiting for transfers between devices: 109 us -> 88.3 us
  between operations: 19.7 us -> 6.24 us
  local copies, waits for them, and re-layouts: 17 us -> 26.7 us
  starting transfers between devices: 20.7 us -> 25.6 us
    all_gather x2 -> x0, waiting for transfers between devices: 41.4 us -> none  [gather(): values = lax.all_gather(values, name, axis=0, tiled=True)]
    ppermute x0 -> x3, waiting for transfers between devices: none -> 20.5 us  [gather(): lax.ppermute(values, name, [(i, (i + size - k) % size) for i in range(siz...]
    unnamed x22 -> x29, local copies, waits for them, and re-layouts: 0.81 us -> 7.15 us
    ppermute x0 -> x3, starting transfers between devices: none -> 4.87 us  [gather(): lax.ppermute(values, name, [(i, (i + size - k) % size) for i in range(siz...]
    all_gather x1 -> x2, blocking collectives: 26.9 us -> 27.6 us  [gather(): values = lax.all_gather(values, name, axis=0, tiled=True)]
  transfers between devices with their start and end apart: 4 -> 5, of which waited for: 4 -> 4; matrix products, arithmetic and copies ran while one was open for 1% -> 2% of each run, Pallas kernels for 0% -> 0%
where the time goes in v8:
time: 200 us; the launch traced here: 198 us
  waiting for transfers between devices  88.3 us (44%)
  blocking collectives  44.8 us (22%)
  local copies, waits for them, and re-layouts  26.7 us (13%)
  starting transfers between devices  25.6 us (13%)
  other arithmetic  6.4 us (3%)
  between operations  6.24 us (3%)
    all_to_all x1, waiting for transfers between devices, local(): got = lax.all_to_all(send, DP, 0, 0, tiled=True)  60.2 us
    all_gather x2, blocking collectives, gather(): values = lax.all_gather(values, name, axis=0, tiled=True)  27.6 us
    ppermute x3, waiting for transfers between devices, gather(): lax.ppermute(values, name, [(i, (i + size - k) % size) for i in range(siz...  20.5 us
    psum x1, blocking collectives, local(): packed = lax.psum(packed, 'tensor')  17.2 us
    all_to_all x1, starting transfers between devices, local(): got = lax.all_to_all(send, DP, 0, 0, tiled=True)  12.2 us
    all_to_all x1, starting transfers between devices, local(): squares = jnp.sum(lax.all_to_all(spread, DP, 0, 0, tiled=True))  8.49 us
    all_to_all x1, waiting for transfers between devices, local(): squares = jnp.sum(lax.all_to_all(spread, DP, 0, 0, tiled=True))  7.55 us
    unnamed x29, local copies, waits for them, and re-layouts  7.15 us
  transfers between devices with their start and end apart: 5, of which 4 were waited for; matrix products, arithmetic and copies ran while one was open for 2% of the time, Pallas kernels for 0%

profile of v8, /device:TPU:4, one launch (start us, length us, event | category | flops | bytes accessed | tf_op | source)
XLA Modules:
  0.0 198.0 jit_solution(18282332297180285942)
XLA Ops:
  0.7 1.0 copy.75
  1.6 5.1 %copy.74 = bf16[512,2,1024]{2,1,0:T(2,128)(2,1)} copy(bf16[512,2,1024]{2,0,1:T(8,128)(2,1)} %bitcast.80) | data formatting | bytes 4194304 | tf_op jit(solution)/shard_map/transpose | solution.py:62
  6.7 3.3 %concatenate.21 = bf16[64,8,2048]{2,1,0:T(8,128)(2,1)S(1)} reshape(bf16[512,2,1024]{2,1,0:T(2,128)(2,1)} %copy.74) | data formatting | bytes 4194304 | tf_op jit(solution)/shard_map/concatenate | solution.py:63
  10.0 1.8 pad_maximum_fusion
  11.8 0.0 copy-start.5
  11.9 12.2 %all-to-all-start = ((bf16[64,8,2596]{2,1,0:T(8,128)(2,1)}), bf16[64,8,2596]{2,1,0:T(8,128)(2,1)S(1)}, u32[]{:S(2)}, u32[]{:S(2)}) async-start(bf16[64,8,2596]{2,1,0:T(8,128)(2,1)} %pad_maximum_fusion), calls=%async_computation | async-start | bytes 5505024 | tf_op jit(solution)/shard_map/all_to_all | solution.py:64
  26.1 60.2 %all-to-all-done = bf16[64,8,2596]{2,1,0:T(8,128)(2,1)S(1)} async-done(((bf16[64,8,2596]{2,1,0:T(8,128)(2,1)}), bf16[64,8,2596]{2,1,0:T(8,128)(2,1)S(1)}, u32[]{:S(2)}, u32[]{:S(2)}) %all-to-all-start) | async-done | bytes 2658336 | tf_op jit(solution)/shard_map/all_to_all | solution.py:64
  86.3 0.5 convert_reduce_fusion
  86.8 0.6 multiply_reduce_fusion
  87.4 0.6 multiply_reduce_fusion.1
  89.3 0.1 constant_dynamic-update-slice_fusion.3
  89.4 0.1 constant_dynamic-update-slice_fusion.2
  89.5 0.1 constant_dynamic-update-slice_fusion.1
  89.6 17.2 %psum.7 = f32[5,36,8]{1,2,0:T(8,128)S(1)} all-reduce(f32[5,36,8]{1,2,0:T(8,128)S(1)} %constant_dynamic-update-slice_fusion), channel_id=1, replica_groups=mesh['dp_x'=4,'dp_z'=8,'dp_core'=2,'tensor'=4] {'tensor'}, use_global_device_ids=true, to_apply=%region_3.4 | all-reduce | flops 1440 | bytes 11520 | tf_op jit(solution)/shard_map/psum | solution.py:85
  106.8 0.6 multiply_reduce_fusion.2
  107.4 0.5 slice.63
  109.2 0.6 broadcast_in_dim.28
  109.8 8.5 %all-to-all-start.1 = ((f32[64,1,1]{2,1,0:T(1,128)}), f32[64,1,1]{2,1,0:T(1,128)S(1)}, u32[]{:S(2)}, u32[]{:S(2)}) async-start(f32[64,1,1]{2,1,0:T(1,128)} %broadcast_in_dim.28), calls=%async_computation.1 | async-start | bytes 65536 | tf_op jit(solution)/shard_map/all_to_all | solution.py:91
  118.4 7.6 %all-to-all-done.1 = f32[64,1,1]{2,1,0:T(1,128)S(1)} async-done(((f32[64,1,1]{2,1,0:T(1,128)}), f32[64,1,1]{2,1,0:T(1,128)S(1)}, u32[]{:S(2)}, u32[]{:S(2)}) %all-to-all-start.1) | async-done | bytes 288 | tf_op jit(solution)/shard_map/all_to_all | solution.py:91
  126.0 0.7 reduce_sum.49
  127.5 0.6 fusion.7
  128.1 0.7 fusion.9
  128.8 1.9 all_gather.6
  130.7 25.7 %all_gather.7 = bf16[128,2596]{1,0:T(8,128)(2,1)S(1)} all-gather(bf16[16,2596]{1,0:T(8,128)(2,1)S(1)} %all_gather.6), channel_id=1, replica_groups=mesh['dp_x'=4,'dp_z'=8,'dp_core'=2,'tensor'=4] {'dp_z'}, dimensions={0}, use_global_device_ids=true | all-gather | bytes 747648 | tf_op jit(solution)/shard_map/all_gather | solution.py:120
  156.4 0.3 copy.77
  156.7 1.2 collective-permute-start.2
  158.0 1.7 collective-permute-start.1
  159.6 2.0 collective-permute-start
  161.6 0.6 constant_dynamic-slice_fusion.2
  162.2 0.6 constant_dynamic-slice_fusion
  162.7 0.9 bitcast_dynamic-update-slice_fusion.4
  163.6 10.4 %collective-permute-done.2 = bf16[128,2596]{0,1:T(8,128)(2,1)S(1)} collective-permute-done((bf16[128,2596]{0,1:T(8,128)(2,1)S(1)}, bf16[128,2596]{0,1:T(8,128)(2,1)S(1)}, u32[]{:S(2)}, u32[]{:S(2)}) %collective-permute-start.2) | collective-permute-done | bytes 664608 | tf_op jit(solution)/shard_map/ppermute | solution.py:124
  174.0 0.3 copy.82
  174.4 10.2 %collective-permute-done = bf16[128,2596]{0,1:T(8,128)(2,1)} collective-permute-done((bf16[128,2596]{0,1:T(8,128)(2,1)S(1)}, bf16[128,2596]{0,1:T(8,128)(2,1)}, u32[]{:S(2)}, u32[]{:S(2)}) %collective-permute-start) | collective-permute-done | bytes 664608 | tf_op jit(solution)/shard_map/ppermute | solution.py:124
  184.5 1.4 copy.78
  186.0 0.9 bitcast_dynamic-update-slice_fusion.2
  186.9 0.3 copy.80
  187.2 0.9 bitcast_dynamic-update-slice_fusion
  188.1 0.9 constant_dynamic-update-slice_fusion.6
  189.0 0.9 bitcast_dynamic-update-slice_fusion.5
  189.9 0.9 bitcast_dynamic-update-slice_fusion.3
  190.9 0.9 bitcast_dynamic-update-slice_fusion.1
  191.8 0.9 constant_dynamic-update-slice_fusion.5
  192.7 2.0 constant_dynamic-slice_fusion.3
  194.7 0.8 slice.68
  195.5 0.3 slice.69
  195.8 0.7 copy.85
  196.5 1.5 copy.89
  (31 shorter events, 0.1 us)
Async XLA Ops:
  0.6 9.4 %copy-start = (bf16[1,1,512,512]{3,2,1,0:T(8,128)(2,1)S(1)}, bf16[1,1,512,512]{3,2,1,0:T(8,128)(2,1)}, u32[]{:S(2)}) copy-start(bf16[1,1,512,512]{3,2,1,0:T(8,128)(2,1)} %param.17) | copy-start | bytes 1572868
  11.8 77.5 %copy-start.7 = (f32[36,2]{0,1:T(2,128)S(1)}, f32[36,2]{0,1:T(2,128)}, u32[]{:S(2)}) copy-start(f32[36,2]{0,1:T(2,128)} %param.26) | copy-start | bytes 868
  11.8 77.6 %copy-start.8 = (f32[36,2]{0,1:T(2,128)S(1)}, f32[36,2]{0,1:T(2,128)}, u32[]{:S(2)}) copy-start(f32[36,2]{0,1:T(2,128)} %param.27) | copy-start | bytes 868
  11.8 77.7 %copy-start.9 = (f32[36,2]{0,1:T(2,128)S(1)}, f32[36,2]{0,1:T(2,128)}, u32[]{:S(2)}) copy-start(f32[36,2]{0,1:T(2,128)} %param.28) | copy-start | bytes 868
  11.8 115.6 %copy-start.4 = (f32[8,512]{1,0:T(8,128)S(1)}, f32[8,512]{1,0:T(8,128)}, u32[]{:S(2)}) copy-start(f32[8,512]{1,0:T(8,128)} %param.20) | copy-start | bytes 49156
  11.8 115.6 %copy-start.5 = (f32[8,512]{1,0:T(8,128)S(1)}, f32[8,512]{1,0:T(8,128)}, u32[]{:S(2)}) copy-start(f32[8,512]{1,0:T(8,128)} %param.22) | copy-start | bytes 49156
  11.8 115.6 %copy-start.6 = (f32[8,512]{1,0:T(8,128)S(1)}, f32[8,512]{1,0:T(8,128)}, u32[]{:S(2)}) copy-start(f32[8,512]{1,0:T(8,128)} %param.21) | copy-start | bytes 49156
  11.8 116.3 %copy-start.1 = (f32[2,8,1024]{2,1,0:T(8,128)S(1)}, f32[2,8,1024]{2,1,0:T(8,128)}, u32[]{:S(2)}) copy-start(f32[2,8,1024]{2,1,0:T(8,128)} %param.23) | copy-start | bytes 196612
  11.8 116.3 %copy-start.2 = (f32[2,8,1024]{2,1,0:T(8,128)S(1)}, f32[2,8,1024]{2,1,0:T(8,128)}, u32[]{:S(2)}) copy-start(f32[2,8,1024]{2,1,0:T(8,128)} %param.25) | copy-start | bytes 196612
  11.8 116.3 %copy-start.3 = (f32[2,8,1024]{2,1,0:T(8,128)S(1)}, f32[2,8,1024]{2,1,0:T(8,128)}, u32[]{:S(2)}) copy-start(f32[2,8,1024]{2,1,0:T(8,128)} %param.24) | copy-start | bytes 196612
  11.9 74.4 %all-to-all-start = ((bf16[64,8,2596]{2,1,0:T(8,128)(2,1)}), bf16[64,8,2596]{2,1,0:T(8,128)(2,1)S(1)}, u32[]{:S(2)}, u32[]{:S(2)}) async-start(bf16[64,8,2596]{2,1,0:T(8,128)(2,1)} %pad_maximum_fusion), calls=%async_computation | async-start | bytes 5505024 | tf_op jit(solution)/shard_map/all_to_all | solution.py:64
  109.8 16.1 %all-to-all-start.1 = ((f32[64,1,1]{2,1,0:T(1,128)}), f32[64,1,1]{2,1,0:T(1,128)S(1)}, u32[]{:S(2)}, u32[]{:S(2)}) async-start(f32[64,1,1]{2,1,0:T(1,128)} %broadcast_in_dim.28), calls=%async_computation.1 | async-start | bytes 65536 | tf_op jit(solution)/shard_map/all_to_all | solution.py:91
  156.7 17.3 %collective-permute-start.2 = (bf16[128,2596]{0,1:T(8,128)(2,1)S(1)}, bf16[128,2596]{0,1:T(8,128)(2,1)S(1)}, u32[]{:S(2)}, u32[]{:S(2)}) collective-permute-start(bf16[128,2596]{0,1:T(8,128)(2,1)S(1)} %copy.77), channel_id=1, source_target_pairs={{0,64},{64,128},{128,192},{192,0},{1,65},{65,129},{129,193},{193,1... | collective-permute-start | bytes 1993736 | tf_op jit(solution)/shard_map/ppermute | solution.py:124
  158.0 28.9 %collective-permute-start.1 = (bf16[128,2596]{0,1:T(8,128)(2,1)S(1)}, bf16[128,2596]{0,1:T(8,128)(2,1)S(1)}, u32[]{:S(2)}, u32[]{:S(2)}) collective-permute-start(bf16[128,2596]{0,1:T(8,128)(2,1)S(1)} %copy.77), channel_id=1, source_target_pairs={{0,128},{64,192},{128,0},{192,64},{1,129},{65,193},{129,1},{193,65... | collective-permute-start | bytes 1993736 | tf_op jit(solution)/shard_map/ppermute | solution.py:124
  159.6 24.9 %collective-permute-start = (bf16[128,2596]{0,1:T(8,128)(2,1)S(1)}, bf16[128,2596]{0,1:T(8,128)(2,1)}, u32[]{:S(2)}, u32[]{:S(2)}) collective-permute-start(bf16[128,2596]{0,1:T(8,128)(2,1)S(1)} %copy.77), channel_id=1, source_target_pairs={{0,192},{64,0},{128,64},{192,128},{1,193},{65,1},{129,65},{193,129... | collective-permute-start | bytes 1993736 | tf_op jit(solution)/shard_map/ppermute | solution.py:124
